TPU v7x, 512 devices: a whole 4x8x8 slice. The times are simulated.
512 devices in a mesh: dp: 64 (over x, z, core), grp: 8 (over y).
Axes of the slice: x: 4, y: 8, z: 8, core: 2. Of those that a mesh axis runs over, the one named last changes fastest.
Arguments:
- tokens: bfloat16 [262144, 1024], P(('dp', 'grp')), may hold values from -24 to 24
- weight: bfloat16 [1024, 512], replicated, may hold values from -0.1875 to 0.1875
- captions: bfloat16 [65536, 512], P(('dp', 'grp')), may hold values from -400 to 400
- block_owner: int32 [64], replicated, may hold values from 0 to 63, each once
- confusable: int32 [64, 14], replicated, may hold values from 0 to 63, as said below
- counts: int32 [64], replicated, may hold values from 1 to 14, as said below
Outputs:
- clip_loss: float32 [65536], P(('dp', 'grp'))
- grad_pooled: float32 [65536, 512], P(('dp', 'grp'))
- grad_w: float32 [1024, 512], P('dp', 'grp')
Inputs may be any that keep to these rules, and one draw needn't show every extreme that they name: `block_owner`: a permutation: each dp index holds exactly one caption group. `confusable`: row p holds 14 distinct caption group ids, none equal to p; only the first counts[p] entries are used. `counts`: some clip group uses all 14 entries.
All inputs are finite; a program needn't handle non-finite values.
Results may differ from a plain program's by a relative error of at most 0.035.
The roundings to bfloat16 on the way count: a program that leaves them out, or rounds other values in their place, can miss the bound.
Values may be sent and summed in bfloat16 or wider, within the bound.
No kernel may reach another device: no remote copies, remote signals or barrier semaphores. Data moves between devices by JAX's collectives and lax.ppermute only.
A program may use at most 64 MiB of HBM per device.

v0:
```python
import jax
import jax.numpy as jnp
from jax import lax
from jax.sharding import PartitionSpec as P

SCORE_SCALE = 2.0
EPSILON = 1e-06
FLOOR = -1e30


def combined_all(part, axis, combine):
    gathered = jax.tree.map(lambda a: lax.all_gather(a, axis), part)

    def take(source):
        return jax.tree.map(lambda a: lax.dynamic_index_in_dim(a, source, 0, False), gathered)

    return lax.fori_loop(
        1, lax.axis_size(axis), lambda source, state: combine(state, take(source)), take(0)
    )


def combine_rows(left_pair, right_pair):
    row_top = jnp.maximum(left_pair[0], right_pair[0])
    row_total = left_pair[1] * jnp.exp(left_pair[0] - row_top) + right_pair[1] * jnp.exp(
        right_pair[0] - row_top
    )
    return (row_top, row_total)


def on_device(tokens, weight, captions, block_owner, confusable, counts):
    members = lax.axis_size("grp")
    groups = lax.axis_size("dp")
    group_index = lax.axis_index("dp")
    member_index = lax.axis_index("grp")
    block_rows = captions.shape[0]
    width = captions.shape[1]
    frames = tokens.shape[0] // block_rows
    factor = SCORE_SCALE / width**0.5
    projected = jnp.dot(tokens, weight, preferred_element_type=jnp.float32)
    activated = jax.nn.gelu(projected)
    pooled = jnp.mean(activated.reshape(block_rows, frames, width), axis=1)
    inverse_rms = lax.rsqrt(jnp.mean(pooled * pooled, axis=-1, keepdims=True) + EPSILON)
    unit_rows = pooled * inverse_rms
    embedded = unit_rows.astype(jnp.bfloat16)
    group_clips = lax.all_gather(embedded, "grp", axis=0, tiled=True)
    listed = jnp.concatenate([jnp.arange(groups, dtype=jnp.int32)[:, None], confusable], axis=1)
    slot_count = listed.shape[1] + 1
    usable_all = jnp.arange(listed.shape[1], dtype=jnp.int32)[None, :] < (1 + counts)[:, None]
    sources = block_owner[listed[group_index]]
    held_group = jnp.sum(
        jnp.where(block_owner == group_index, jnp.arange(groups, dtype=jnp.int32), 0)
    )
    wanted = jnp.any((listed == held_group) & usable_all, axis=1)
    outgoing = jnp.where(wanted[:, None, None], captions[None], jnp.zeros((), jnp.bfloat16))
    incoming = lax.all_to_all(outgoing, "dp", split_axis=0, concat_axis=0, tiled=True)
    fetched = jnp.take(incoming, sources, axis=0)
    caption_slots = jnp.concatenate([captions[None], fetched], axis=0)
    usable = jnp.arange(slot_count, dtype=jnp.int32) < 2 + counts[group_index]
    scores = factor * jnp.einsum(
        "re,sce->rsc", group_clips, caption_slots, preferred_element_type=jnp.float32
    )
    scores = jnp.where(usable[None, :, None], scores, FLOOR)
    row_top = jnp.max(scores, axis=(1, 2))
    row_total = jnp.sum(jnp.exp(scores - row_top[:, None, None]), axis=(1, 2))
    row_top, row_total = combined_all((row_top, row_total), "grp", combine_rows)
    logsum = row_top + jnp.log(row_total)
    own_start = member_index * block_rows
    own_scores = lax.dynamic_slice_in_dim(scores[:, 1, :], own_start, block_rows, 0)
    positive = jnp.diagonal(own_scores)
    clip_loss = lax.dynamic_slice_in_dim(logsum, own_start, block_rows, 0) - positive
    weights = jnp.exp(scores - logsum[:, None, None]).astype(jnp.bfloat16)
    partial_sums = jnp.einsum(
        "rsc,sce->re", weights, caption_slots, preferred_element_type=jnp.float32
    )
    own_rows = lax.dynamic_slice_in_dim(partial_sums, own_start, block_rows, 0) - caption_slots[
        1
    ].astype(jnp.float32)
    partial_sums = lax.dynamic_update_slice_in_dim(partial_sums, own_rows, own_start, 0)
    grad_unit = factor * lax.psum_scatter(
        partial_sums.astype(jnp.bfloat16), "grp", scatter_dimension=0, tiled=True
    ).astype(jnp.float32)
    grad_pooled = inverse_rms * (
        grad_unit - unit_rows * jnp.mean(grad_unit * unit_rows, axis=-1, keepdims=True)
    )
    spread = jnp.broadcast_to(
        grad_pooled[:, None, :] / frames, (block_rows, frames, width)
    ).reshape(block_rows * frames, width)
    gelu_out, pullback = jax.vjp(jax.nn.gelu, projected)
    grad_projected = pullback(spread)[0].astype(jnp.bfloat16)
    scale_down = 1.0 / (groups * members) ** 0.5
    contract = (((0,), (0,)), ((), ()))
    shard_rows = lax.psum_scatter(
        scale_down
        * lax.dot_general(tokens, grad_projected, contract, preferred_element_type=jnp.float32),
        "dp",
        scatter_dimension=0,
        tiled=True,
    )
    grad_w = lax.psum_scatter(
        shard_rows.astype(jnp.bfloat16), "grp", scatter_dimension=1, tiled=True
    ).astype(jnp.float32)
    return (clip_loss, grad_pooled, grad_w)


def solution(mesh):
    in_specs = (P(("dp", "grp"), None), P(), P(("dp", "grp"), None), P(), P(), P())
    out_specs = (P(("dp", "grp")), P(("dp", "grp"), None), P("dp", "grp"))
    return jax.shard_map(
        on_device, mesh=mesh, in_specs=in_specs, out_specs=out_specs, check_vma=False
    )
```

profile of v0, /device:TPU:1, one launch (start us, length us, event | category | flops | bytes accessed | tf_op | source)
XLA Modules:
  0.0 527.9 jit_solution(2144286295300128522)
XLA Ops:
  7.2 0.0 copy-start
  7.2 1.4 fusion.24
  8.6 1.4 fusion.23
  10.0 4.7 broadcast_select_fusion
  14.7 0.0 copy-start.6
  14.7 15.2 %all-to-all-start = ((bf16[64,128,512]{2,1,0:T(8,128)(2,1)}), bf16[64,128,512]{2,1,0:T(8,128)(2,1)}, u32[]{:S(2)}, u32[]{:S(2)}) async-start(bf16[64,128,512]{2,1,0:T(8,128)(2,1)} %broadcast_select_fusion), calls=%async_computation | async-start | bytes 16777216 | tf_op jit(solution)/shard_map/all_to_all | solution.py:55
  29.9 0.0 all-gather.4.cloned.1.call-start
  29.9 0.0 copy-done
  29.9 0.0 copy-done.6
  29.9 1.8 multiply_multiply_fusion.2
  31.7 0.0 copy-start.5
  31.7 0.0 copy-start.4
  31.7 0.0 copy-start.1
  31.7 0.3 reshape.86
  32.0 0.6 reduce_sum.45
  32.7 0.1 multiply_reduce_fusion.1
  32.8 0.8 multiply_convert_fusion
  33.5 0.0 all-gather.4.cloned.1.call-update
  33.6 0.0 reduce-scatter.6.cloned.1.call-start
  33.6 0.0 copy-done.5
  33.6 0.6 dynamic_slice.44
  34.2 0.0 copy-done.4
  34.2 0.2 fusion.21
  34.4 0.0 copy-done.1
  34.4 0.7 gather_fusion
  35.8 179.8 %all-to-all-done = bf16[64,128,512]{2,1,0:T(8,128)(2,1)} async-done(((bf16[64,128,512]{2,1,0:T(8,128)(2,1)}), bf16[64,128,512]{2,1,0:T(8,128)(2,1)}, u32[]{:S(2)}, u32[]{:S(2)}) %all-to-all-start) | async-done | bytes 8388640 | tf_op jit(solution)/shard_map/all_to_all | solution.py:55
  215.6 4.1 gather_fusion.1
  219.7 0.0 copy-start.3
  219.7 1.6 broadcast_select_fusion.1
  221.3 0.0 all-gather.4.cloned.1.call-done
  221.3 0.0 copy-done.3
  221.3 7.6 %fusion.35 = (f32[1024]{0:T(1024)S(1)}, f32[1024,16,128]{0,2,1:T(8,128)}) fusion(bf16[15,128,512]{2,1,0:T(8,128)(2,1)} %broadcast_select_fusion.1, bf16[1,128,512]{2,1,0:T(8,128)(2,1)S(1)} %bitcast.40, bf16[1024,512]{1,0:T(8,128)(2,1)} %all-gather.4.cloned.1.call-done, pred[16]{0:T(512)(128)(4,1)S(1)} %iota_compare_fusion.1), kind=kOutput, calls=%fused_computation.77 | convolution fusion | flops 2157968384 | bytes 11538448 | tf_op jit(solution)/shard_map/re,sce->rsc/dot_general | solution.py:59
  228.9 19.7 %all-gather = f32[8192]{0:T(1024)S(1)} all-gather(f32[1024]{0:T(1024)S(1)} %get-tuple-element.167), channel_id=2, replica_groups=mesh['dp'=64,'grp'=8] {'grp'}, dimensions={0}, use_global_device_ids=true | all-gather | bytes 36864 | tf_op jit(solution)/shard_map/all_gather | solution.py:12
  248.6 0.0 copy-start.2
  248.6 4.7 exponential_reduce_fusion
  253.3 18.1 %all-gather.1 = f32[8192]{0:T(1024)S(1)} all-gather(f32[1024]{0:T(1024)S(1)} %exponential_reduce_fusion), channel_id=3, replica_groups=mesh['dp'=64,'grp'=8] {'grp'}, dimensions={0}, use_global_device_ids=true | all-gather | bytes 36864 | tf_op jit(solution)/shard_map/all_gather | solution.py:12
  271.4 0.4 while.17
  271.8 0.0 copy-done.2
  271.8 5.8 %fusion.2 = f32[1024,512]{1,0:T(8,128)S(1)} fusion(f32[1024,16,128]{0,2,1:T(8,128)} %get-tuple-element.168, f32[1024]{0:T(1024)S(1)} %log_add_fusion, bf16[15,128,512]{2,1,0:T(8,128)(2,1)S(1)} %copy-done.2, bf16[1,128,512]{2,1,0:T(8,128)(2,1)S(1)} %bitcast.41), kind=kOutput, calls=%fused_computation.15 | convolution fusion | flops 2152726528 | bytes 12587008 | tf_op jit(solution)/shard_map/rsc,sce->re/dot_general | solution.py:72
  277.6 1.2 convert_element_type.31
  278.8 0.0 reduce-scatter.6.cloned.1.call-update
  278.8 0.2 reduce-scatter.10.cloned.1.call-start
  279.1 44.2 %reduce-scatter.6.cloned.1.call-done = bf16[128,512]{1,0:T(8,128)(2,1)} async-done(((bf16[1024,512]{1,0:T(8,128)(2,1)}), bf16[128,512]{1,0:T(8,128)(2,1)}) %reduce-scatter.6.cloned.1.call-update) | async-done | bytes 131088 | tf_op jit(solution)/shard_map/reduce_scatter | solution.py:79
  323.3 1.1 multiply_reduce_fusion
  324.4 1.7 broadcast_multiply_fusion
  326.2 0.2 broadcast_in_dim.79
  326.3 1.4 reshape.87
  327.8 2.8 multiply_bitcast_fusion
  330.6 1.9 copy.16
  332.5 0.0 reduce-scatter.10.cloned.1.call-update
  332.5 0.0 reduce-scatter.8.cloned.1.call-start
  332.6 1.1 slice.20
  333.7 1.3 gather_fusion.2
  335.0 145.8 %reduce-scatter.10.cloned.1.call-done = f32[16,512]{1,0:T(8,128)} async-done(((f32[1024,512]{1,0:T(8,128)}), f32[16,512]{1,0:T(8,128)}) %reduce-scatter.10.cloned.1.call-update) | async-done | bytes 32784
  480.7 1.5 copy.17
  482.2 0.0 reduce-scatter.8.cloned.1.call-update
  482.3 0.6 dynamic-slice_subtract_fusion
  482.8 37.1 %reduce-scatter.8.cloned.1.call-done = bf16[16,64]{0,1:T(8,128)(2,1)} async-done(((bf16[16,512]{0,1:T(8,128)(2,1)}), bf16[16,64]{0,1:T(8,128)(2,1)}) %reduce-scatter.8.cloned.1.call-update) | async-done | bytes 2064 | tf_op jit(solution)/shard_map/reduce_scatter | solution.py:99
  519.9 1.4 copy.14
  (31 shorter events, 0.3 us)
Async XLA Ops:
  7.2 22.7 %copy-start = (bf16[512,1024]{1,0:T(8,128)(2,1)S(1)}, bf16[512,1024]{1,0:T(8,128)(2,1)}, u32[]{:S(2)}) copy-start(bf16[512,1024]{1,0:T(8,128)(2,1)} %param.8) | copy-start | bytes 3145732
  14.7 15.2 %copy-start.6 = (bf16[1024,512]{1,0:T(8,128)(2,1)S(1)}, bf16[1024,512]{1,0:T(8,128)(2,1)}, u32[]{:S(2)}) copy-start(bf16[1024,512]{1,0:T(8,128)(2,1)} %param.9) | copy-start | bytes 3145732
  14.7 200.9 %all-to-all-start = ((bf16[64,128,512]{2,1,0:T(8,128)(2,1)}), bf16[64,128,512]{2,1,0:T(8,128)(2,1)}, u32[]{:S(2)}, u32[]{:S(2)}) async-start(bf16[64,128,512]{2,1,0:T(8,128)(2,1)} %broadcast_select_fusion), calls=%async_computation | async-start | bytes 16777216 | tf_op jit(solution)/shard_map/all_to_all | solution.py:55
  29.9 191.4 %all-gather.4.cloned.1.call-start = ((), (), s32[]{:S(2)}) async-start(), calls=%async_computation.4 | async-start | bytes 1179648 | tf_op jit(solution)/shard_map/all_gather | solution.py:45
  31.7 1.9 copy-start.5
  31.7 2.5 copy-start.4
  31.7 2.7 copy-start.1
  33.6 289.8 %reduce-scatter.6.cloned.1.call-start = ((), (), s32[]{:S(2)}) async-start(), calls=%async_computation.5 | async-start | bytes 1179648 | tf_op jit(solution)/shard_map/reduce_scatter | solution.py:79
  219.7 1.6 copy-start.3
  248.6 23.2 %copy-start.2 = (bf16[15,128,512]{2,1,0:T(8,128)(2,1)S(1)}, bf16[15,128,512]{2,1,0:T(8,128)(2,1)}, u32[]{:S(2)}) copy-start(bf16[15,128,512]{2,1,0:T(8,128)(2,1)} %broadcast_select_fusion.1) | copy-start | bytes 5898244
  278.8 201.9 %reduce-scatter.10.cloned.1.call-start = ((), (), s32[]{:S(2)}) async-start(), calls=%async_computation.7 | async-start | bytes 2129920
  332.5 187.4 %reduce-scatter.8.cloned.1.call-start = ((), (), s32[]{:S(2)}) async-start(), calls=%async_computation.6 | async-start | bytes 147456 | tf_op jit(solution)/shard_map/reduce_scatter | solution.py:99
Sparse Core Ops, SparseCore 0:
  33.7 38.1 all-gather.3
  279.0 44.3 reduce-scatter.5
  332.6 148.0 reduce-scatter.9
  483.6 36.2 reduce-scatter.7
where the time goes:
time: 533 us; the launch traced here: 528 us
  waiting for transfers between devices  407 us (76%)
  blocking collectives  37.8 us (7%)
  other arithmetic  20.3 us (4%)
  matrix products  17.9 us (3%)
  starting transfers between devices  15.5 us (3%)
  between operations  14.6 us (3%)
  local copies, waits for them, and re-layouts  14.5 us (3%)
    all_to_all x1, waiting for transfers between devices, on_device(): lax.all_to_all(outgoing, 'dp', split_axis=0, concat_axis=0, tiled=True)  180 us
    unnamed x5, waiting for transfers between devices  146 us
    reduce_scatter x1, waiting for transfers between devices, on_device(): lax.psum_scatter(partial_sums.astype(jnp.bfloat16), 'grp', scatter_dimens...  44.2 us
    all_gather x2, blocking collectives, combined_all(): gathered = jax.tree.map(lambda a: lax.all_gather(a, axis), part)  37.8 us
    reduce_scatter x1, waiting for transfers between devices, on_device(): lax.psum_scatter(shard_rows.astype(jnp.bfloat16), 'grp', scatter_dimensio...  37.1 us
    all_to_all x1, starting transfers between devices, on_device(): lax.all_to_all(outgoing, 'dp', split_axis=0, concat_axis=0, tiled=True)  15.2 us
  transfers between devices with their start and end apart: 5, of which 4 were waited for; matrix products, arithmetic and copies ran while one was open for 3% of the time, Pallas kernels for 0%

commit v1 on v0

v1 whole, which is shorter than its diff:
```python
import jax
import jax.numpy as jnp
from jax import lax
from jax.sharding import PartitionSpec as P

SCORE_SCALE = 2.0
EPSILON = 1e-06
FLOOR = -1e30


def gather_ring(part, axis):
    size = lax.axis_size(axis)
    me = lax.axis_index(axis)
    received = [part]
    for shift in range(1, size):
        pairs = [(i, (i + shift) % size) for i in range(size)]
        received.append(lax.ppermute(part, axis, pairs))
    stacked = jnp.stack(received)
    order = (me - jnp.arange(size, dtype=jnp.int32)) % size
    return jnp.take(stacked, order, axis=0)


def reduce_blocks(blocks, axis):
    swapped = lax.all_to_all(blocks, axis, 0, 0, tiled=True)
    return jnp.sum(swapped.astype(jnp.float32), axis=0)


def on_device(tokens, weight, captions, block_owner, confusable, counts):
    members = lax.axis_size("grp")
    groups = lax.axis_size("dp")
    group_index = lax.axis_index("dp")
    member_index = lax.axis_index("grp")
    block_rows = captions.shape[0]
    width = captions.shape[1]
    depth = tokens.shape[1]
    frames = tokens.shape[0] // block_rows
    factor = SCORE_SCALE / width**0.5
    every_block = lax.all_gather(captions, "dp", axis=0, tiled=False)
    projected = jnp.dot(tokens, weight, preferred_element_type=jnp.float32)
    activated = jax.nn.gelu(projected)
    pooled = jnp.mean(activated.reshape(block_rows, frames, width), axis=1)
    inverse_rms = lax.rsqrt(jnp.mean(pooled * pooled, axis=-1, keepdims=True) + EPSILON)
    unit_rows = pooled * inverse_rms
    embedded = unit_rows.astype(jnp.bfloat16)
    group_clips = gather_ring(embedded, "grp").reshape(members * block_rows, width)
    listed = jnp.concatenate([jnp.arange(groups, dtype=jnp.int32)[:, None], confusable], axis=1)
    slot_count = listed.shape[1] + 1
    sources = block_owner[listed[group_index]]
    fetched = jnp.take(every_block, sources, axis=0)
    caption_slots = jnp.concatenate([captions[None], fetched], axis=0)
    usable = jnp.arange(slot_count, dtype=jnp.int32) < 2 + counts[group_index]
    scores = factor * jnp.einsum(
        "re,sce->rsc", group_clips, caption_slots, preferred_element_type=jnp.float32
    )
    scores = jnp.where(usable[None, :, None], scores, FLOOR)
    row_top = jnp.max(scores, axis=(1, 2))
    row_total = jnp.sum(jnp.exp(scores - row_top[:, None, None]), axis=(1, 2))
    stats = lax.all_gather(jnp.stack([row_top, row_total]), "grp", axis=0, tiled=False)
    row_top = jnp.max(stats[:, 0], axis=0)
    row_total = jnp.sum(stats[:, 1] * jnp.exp(stats[:, 0] - row_top[None]), axis=0)
    logsum = row_top + jnp.log(row_total)
    own_start = member_index * block_rows
    own_scores = lax.dynamic_slice_in_dim(scores[:, 1, :], own_start, block_rows, 0)
    positive = jnp.diagonal(own_scores)
    clip_loss = lax.dynamic_slice_in_dim(logsum, own_start, block_rows, 0) - positive
    weights = jnp.exp(scores - logsum[:, None, None]).astype(jnp.bfloat16)
    partial_sums = jnp.einsum(
        "rsc,sce->re", weights, caption_slots, preferred_element_type=jnp.float32
    )
    own_rows = lax.dynamic_slice_in_dim(partial_sums, own_start, block_rows, 0) - caption_slots[
        1
    ].astype(jnp.float32)
    partial_sums = lax.dynamic_update_slice_in_dim(partial_sums, own_rows, own_start, 0)
    parts = partial_sums.astype(jnp.bfloat16).reshape(members, block_rows, width)
    grad_unit = factor * reduce_blocks(parts, "grp")
    grad_pooled = inverse_rms * (
        grad_unit - unit_rows * jnp.mean(grad_unit * unit_rows, axis=-1, keepdims=True)
    )
    spread = jnp.broadcast_to(
        grad_pooled[:, None, :] / frames, (block_rows, frames, width)
    ).reshape(block_rows * frames, width)
    gelu_out, pullback = jax.vjp(jax.nn.gelu, projected)
    grad_projected = pullback(spread)[0].astype(jnp.bfloat16)
    scale_down = 1.0 / (groups * members) ** 0.5
    contract = (((0,), (0,)), ((), ()))
    weight_term = scale_down * lax.dot_general(
        tokens, grad_projected, contract, preferred_element_type=jnp.float32
    )
    shard_rows = reduce_blocks(weight_term.reshape(groups, depth // groups, width), "dp")
    columns = width // members
    by_member = jnp.swapaxes(shard_rows.reshape(depth // groups, members, columns), 0, 1)
    grad_w = reduce_blocks(by_member, "grp")
    return (clip_loss, grad_pooled, grad_w)


def solution(mesh):
    in_specs = (P(("dp", "grp"), None), P(), P(("dp", "grp"), None), P(), P(), P())
    out_specs = (P(("dp", "grp")), P(("dp", "grp"), None), P("dp", "grp"))
    return jax.shard_map(
        on_device, mesh=mesh, in_specs=in_specs, out_specs=out_specs, check_vma=False
    )
```

time: 533 us -> 258 us (0.48)
  waiting for transfers between devices: 407 us -> 116 us
  starting transfers between devices: 15.5 us -> 46.1 us
  other arithmetic: 20.3 us -> 7.34 us
  blocking collectives: 37.8 us -> 46.2 us
  matrix products: 17.9 us -> 10.8 us
    unnamed x5 -> x1, waiting for transfers between devices: 146 us -> 0.68 us
    all_to_all x1 -> x2, waiting for transfers between devices: 180 us -> 55 us  [reduce_blocks(): swapped = lax.all_to_all(blocks, axis, 0, 0, tiled=True)]
    reduce_scatter x2 -> x0, waiting for transfers between devices: 81.3 us -> none  [the longest x1 44.2 us: on_device(): lax.psum_scatter(partial_sums.astype(jnp.bfloat16), 'grp', scatter_dimens...]
    all_gather x1, waiting for transfers between devices: 0.01 us -> 50.1 us  [on_device(): every_block = lax.all_gather(captions, 'dp', axis=0, tiled=False)]
    ppermute x0 -> x7, starting transfers between devices: none -> 29.2 us  [gather_ring(): received.append(lax.ppermute(part, axis, pairs))]
    all_to_all x0 -> x1, blocking collectives: none -> 26.9 us  [reduce_blocks(): swapped = lax.all_to_all(blocks, axis, 0, 0, tiled=True)]
    all_gather x2 -> x1, blocking collectives: 37.8 us -> 19.3 us  [on_device(): lax.all_gather(jnp.stack([row_top, row_total]), 'grp', axis=0, tiled=False)]
    ppermute x0 -> x7, waiting for transfers between devices: none -> 10.7 us  [gather_ring(): received.append(lax.ppermute(part, axis, pairs))]
  transfers between devices with their start and end apart: 5 -> 10, of which waited for: 4 -> 6; matrix products, arithmetic and copies ran while one was open for 3% -> 4% of each run, Pallas kernels for 0% -> 0%
where the time goes in v1:
time: 258 us; the launch traced here: 257 us
  waiting for transfers between devices  116 us (45%)
  blocking collectives  46.2 us (18%)
  starting transfers between devices  46.1 us (18%)
  between operations  15.1 us (6%)
  local copies, waits for them, and re-layouts  15 us (6%)
  matrix products  10.8 us (4%)
  other arithmetic  7.34 us (3%)
    all_to_all x2, waiting for transfers between devices, reduce_blocks(): swapped = lax.all_to_all(blocks, axis, 0, 0, tiled=True)  55 us
    all_gather x1, waiting for transfers between devices, on_device(): every_block = lax.all_gather(captions, 'dp', axis=0, tiled=False)  50.1 us
    ppermute x7, starting transfers between devices, gather_ring(): received.append(lax.ppermute(part, axis, pairs))  29.2 us
    all_to_all x1, blocking collectives, reduce_blocks(): swapped = lax.all_to_all(blocks, axis, 0, 0, tiled=True)  26.9 us
    all_gather x1, blocking collectives, on_device(): lax.all_gather(jnp.stack([row_top, row_total]), 'grp', axis=0, tiled=False)  19.3 us
    all_to_all x2, starting transfers between devices, reduce_blocks(): swapped = lax.all_to_all(blocks, axis, 0, 0, tiled=True)  16.8 us
    ppermute x7, waiting for transfers between devices, gather_ring(): received.append(lax.ppermute(part, axis, pairs))  10.7 us
  transfers between devices with their start and end apart: 10, of which 6 were waited for; matrix products, arithmetic and copies ran while one was open for 4% of the time, Pallas kernels for 0%

profile of v1, /device:TPU:1, one launch (start us, length us, event | category | flops | bytes accessed | tf_op | source)
XLA Modules:
  0.0 257.0 jit_solution(498658599213445769)
XLA Ops:
  7.2 0.0 copy-start
  7.2 0.0 all-gather.5.cloned.1.call-start
  7.2 0.7 all-gather.5.cloned.1.call-update
  7.9 0.5 copy-done
  8.4 3.1 %multiply_multiply_fusion.2 = (f32[512,512]{1,0:T(8,128)S(1)}, f32[512,512]{1,0:T(8,128)}) fusion(bf16[512,1024]{1,0:T(8,128)(2,1)S(1)} %copy-done, bf16[1024,512]{1,0:T(8,128)(2,1)} %param.7), kind=kOutput, calls=%fused_computation.25 | convolution fusion | flops 538968064 | bytes 4194304 | tf_op jit(solution)/shard_map/dot_general | solution.py:39
  11.5 0.3 reshape.221
  11.8 0.6 reduce_sum.74
  12.4 0.1 multiply_reduce_fusion.1
  12.6 0.1 multiply_convert_fusion
  12.7 4.0 %collective-permute-start = (bf16[128,512]{1,0:T(8,128)(2,1)S(1)}, bf16[128,512]{1,0:T(8,128)(2,1)S(1)}, u32[]{:S(2)}, u32[]{:S(2)}) collective-permute-start(bf16[128,512]{1,0:T(8,128)(2,1)S(1)} %multiply_convert_fusion), channel_id=1, source_target_pairs={{0,1},{1,2},{2,3},{3,4},{4,5},{5,6},{6,7},{7,0},{8,9},{9,10},{10,1... | collective-permute-start | bytes 393224 | tf_op jit(solution)/shard_map/ppermute | solution.py:17
  16.7 4.2 %collective-permute-start.1 = (bf16[128,512]{1,0:T(8,128)(2,1)S(1)}, bf16[128,512]{1,0:T(8,128)(2,1)S(1)}, u32[]{:S(2)}, u32[]{:S(2)}) collective-permute-start(bf16[128,512]{1,0:T(8,128)(2,1)S(1)} %multiply_convert_fusion), channel_id=1, source_target_pairs={{0,2},{1,3},{2,4},{3,5},{4,6},{5,7},{6,0},{7,1},{8,10},{9,11},{10,... | collective-permute-start | bytes 393224 | tf_op jit(solution)/shard_map/ppermute | solution.py:17
  20.9 4.6 %collective-permute-start.2 = (bf16[128,512]{1,0:T(8,128)(2,1)S(1)}, bf16[128,512]{1,0:T(8,128)(2,1)S(1)}, u32[]{:S(2)}, u32[]{:S(2)}) collective-permute-start(bf16[128,512]{1,0:T(8,128)(2,1)S(1)} %multiply_convert_fusion), channel_id=1, source_target_pairs={{0,3},{1,4},{2,5},{3,6},{4,7},{5,0},{6,1},{7,2},{8,11},{9,12},{10,... | collective-permute-start | bytes 393224 | tf_op jit(solution)/shard_map/ppermute | solution.py:17
  25.6 3.5 %collective-permute-start.3 = (bf16[128,512]{1,0:T(8,128)(2,1)S(1)}, bf16[128,512]{1,0:T(8,128)(2,1)S(1)}, u32[]{:S(2)}, u32[]{:S(2)}) collective-permute-start(bf16[128,512]{1,0:T(8,128)(2,1)S(1)} %multiply_convert_fusion), channel_id=1, source_target_pairs={{0,4},{1,5},{2,6},{3,7},{4,0},{5,1},{6,2},{7,3},{8,12},{9,13},{10,... | collective-permute-start | bytes 393224 | tf_op jit(solution)/shard_map/ppermute | solution.py:17
  29.1 4.9 %collective-permute-start.4 = (bf16[128,512]{1,0:T(8,128)(2,1)S(1)}, bf16[128,512]{1,0:T(8,128)(2,1)S(1)}, u32[]{:S(2)}, u32[]{:S(2)}) collective-permute-start(bf16[128,512]{1,0:T(8,128)(2,1)S(1)} %multiply_convert_fusion), channel_id=1, source_target_pairs={{0,5},{1,6},{2,7},{3,0},{4,1},{5,2},{6,3},{7,4},{8,13},{9,14},{10,... | collective-permute-start | bytes 393224 | tf_op jit(solution)/shard_map/ppermute | solution.py:17
  34.0 0.6 dynamic_slice.17
  34.6 0.2 fusion.24
  34.8 0.7 gather_fusion.1
  36.2 0.1 broadcast_bitcast_fusion
  36.3 0.1 fusion.20
  36.4 0.0 collective-permute-done
  36.4 5.0 %collective-permute-start.5 = (bf16[128,512]{1,0:T(8,128)(2,1)S(1)}, bf16[128,512]{1,0:T(8,128)(2,1)S(1)}, u32[]{:S(2)}, u32[]{:S(2)}) collective-permute-start(bf16[128,512]{1,0:T(8,128)(2,1)S(1)} %multiply_convert_fusion), channel_id=1, source_target_pairs={{0,6},{1,7},{2,0},{3,1},{4,2},{5,3},{6,4},{7,5},{8,14},{9,15},{10,... | collective-permute-start | bytes 393224 | tf_op jit(solution)/shard_map/ppermute | solution.py:17
  41.4 0.0 collective-permute-done.1
  41.4 3.0 %collective-permute-start.6 = (bf16[128,512]{1,0:T(8,128)(2,1)S(1)}, bf16[128,512]{1,0:T(8,128)(2,1)S(1)}, u32[]{:S(2)}, u32[]{:S(2)}) collective-permute-start(bf16[128,512]{1,0:T(8,128)(2,1)S(1)} %multiply_convert_fusion), channel_id=1, source_target_pairs={{0,7},{1,0},{2,1},{3,2},{4,3},{5,4},{6,5},{7,6},{8,15},{9,8},{10,9... | collective-permute-start | bytes 393224 | tf_op jit(solution)/shard_map/ppermute | solution.py:17
  44.4 0.0 collective-permute-done.2
  44.5 0.0 collective-permute-done.3
  44.5 0.5 collective-permute-done.4
  45.0 6.9 %collective-permute-done.5 = bf16[128,512]{1,0:T(8,128)(2,1)S(1)} collective-permute-done((bf16[128,512]{1,0:T(8,128)(2,1)S(1)}, bf16[128,512]{1,0:T(8,128)(2,1)S(1)}, u32[]{:S(2)}, u32[]{:S(2)}) %collective-permute-start.5) | collective-permute-done | bytes 131104 | tf_op jit(solution)/shard_map/ppermute | solution.py:17
  51.9 3.3 %collective-permute-done.6 = bf16[128,512]{1,0:T(8,128)(2,1)S(1)} collective-permute-done((bf16[128,512]{1,0:T(8,128)(2,1)S(1)}, bf16[128,512]{1,0:T(8,128)(2,1)S(1)}, u32[]{:S(2)}, u32[]{:S(2)}) %collective-permute-start.6) | collective-permute-done | bytes 131104 | tf_op jit(solution)/shard_map/ppermute | solution.py:17
  55.2 0.6 gather_fusion
  55.8 1.2 bitcast_select_fusion
  57.0 50.1 %all-gather.5.cloned.1.call-done = bf16[8192,512]{1,0:T(8,128)(2,1)} async-done(((bf16[128,512]{1,0:T(8,128)(2,1)}), bf16[8192,512]{1,0:T(8,128)(2,1)}) %all-gather.5.cloned.1.call-update) | async-done | bytes 8388624 | tf_op jit(solution)/shard_map/all_gather | solution.py:38
  107.1 4.1 %gather_fusion.2 = bf16[15,128,512]{2,1,0:T(8,128)(2,1)S(1)} fusion(bf16[64,128,512]{2,1,0:T(8,128)(2,1)} %bitcast.79, s32[1024]{0:T(1024)S(1)} %pad_clamp_fusion), kind=kCustom, calls=%fused_computation.2 | custom fusion | bytes 3932220 | tf_op jit(solution)/shard_map/jit(_take)/gather | solution.py:49
  111.2 0.0 copy-start.4
  111.2 0.3 broadcast_select_fusion
  111.5 0.9 copy-done.3
  112.4 2.5 fusion.39
  114.9 1.2 exponential_reduce_fusion
  116.1 19.3 %all-gather.2 = f32[8,2,1024]{2,1,0:T(2,128)S(1)} all-gather(f32[1,2,1024]{2,1,0:T(2,128)S(1)} %maximum_bitcast_fusion), channel_id=3, replica_groups=mesh['dp'=64,'grp'=8] {'grp'}, dimensions={0}, use_global_device_ids=true | all-gather | bytes 73728 | tf_op jit(solution)/shard_map/all_gather | solution.py:58
  135.4 0.1 fusion.38
  135.5 2.4 fusion.2
  137.9 0.1 fusion.18
  137.9 0.1 convert_element_type.35
  138.1 26.9 %all_to_all.15 = bf16[8,128,512]{2,1,0:T(8,128)(2,1)S(1)} all-to-all(bf16[8,128,512]{2,1,0:T(8,128)(2,1)S(1)} %bitcast.78), channel_id=1, replica_groups=mesh['dp'=64,'grp'=8] {'grp'}, dimensions={0} | all-to-all | bytes 2097152 | tf_op jit(solution)/shard_map/all_to_all | solution.py:24
  165.0 0.1 convert_reduce_fusion
  165.2 0.2 multiply_reduce_fusion
  165.4 0.8 broadcast_multiply_fusion
  166.2 0.2 broadcast_in_dim.66
  166.4 1.3 reshape.223
  167.7 2.8 %multiply_bitcast_fusion = f32[1024,512]{0,1:T(8,128)S(1)} fusion(bf16[512,1024]{1,0:T(8,128)(2,1)S(1)} %copy-done, f32[512,512]{1,0:T(8,128)} %get-tuple-element.11, f32[512,512]{1,0:T(8,128)} %reshape.223), kind=kOutput, calls=%fused_computation.10 | convolution fusion | flops 542638080 | bytes 5242880 | tf_op jit(solution)/shard_map/dot_general | solution.py:86
  170.5 1.9 copy.19
  172.4 13.4 %all-to-all-start.1 = ((f32[64,16,512]{2,1,0:T(8,128)}), f32[64,16,512]{2,1,0:T(8,128)S(1)}, u32[]{:S(2)}, u32[]{:S(2)}) async-start(f32[64,16,512]{2,1,0:T(8,128)} %bitcast.77), calls=%async_computation.1 | async-start | bytes 4194304 | tf_op jit(solution)/shard_map/all_to_all | solution.py:24
  185.9 1.1 slice.27
  187.0 1.3 gather_fusion.3
  188.3 48.8 %all-to-all-done.1 = f32[64,16,512]{2,1,0:T(8,128)S(1)} async-done(((f32[64,16,512]{2,1,0:T(8,128)}), f32[64,16,512]{2,1,0:T(8,128)S(1)}, u32[]{:S(2)}, u32[]{:S(2)}) %all-to-all-start.1) | async-done | bytes 2097184 | tf_op jit(solution)/shard_map/all_to_all | solution.py:24
  237.1 0.1 reduce_sum.81
  237.2 0.1 reshape.225
  237.3 0.7 reshape.265
  238.0 3.3 %all-to-all-start.2 = ((f32[8,1,1024]{2,1,0:T(1,128)}), f32[8,1,1024]{2,1,0:T(1,128)S(1)}, u32[]{:S(2)}, u32[]{:S(2)}) async-start(f32[8,1,1024]{2,1,0:T(1,128)} %reshape.265), calls=%async_computation.2 | async-start | bytes 65536 | tf_op jit(solution)/shard_map/all_to_all | solution.py:24
  241.4 0.6 dynamic-slice_subtract_fusion
  242.0 6.2 %all-to-all-done.2 = f32[8,1,1024]{2,1,0:T(1,128)S(1)} async-done(((f32[8,1,1024]{2,1,0:T(1,128)}), f32[8,1,1024]{2,1,0:T(1,128)S(1)}, u32[]{:S(2)}, u32[]{:S(2)}) %all-to-all-start.2) | async-done | bytes 32800 | tf_op jit(solution)/shard_map/all_to_all | solution.py:24
  248.2 0.5 broadcast.321
  248.7 0.7 reduce.3
  249.4 0.1 reshape.266
  249.5 0.6 reduce_sum.82
  (34 shorter events, 0.3 us)
Async XLA Ops:
  7.2 1.2 copy-start
  7.2 99.9 %all-gather.5.cloned.1.call-start = ((), (), s32[]{:S(2)}) async-start(), calls=%async_computation.3 | async-start | bytes 8519680 | tf_op jit(solution)/shard_map/all_gather | solution.py:38
  11.5 22.5 %copy-start.6 = (s32[64]{0:T(128)S(1)}, s32[64]{0:T(128)}, u32[]{:S(2)}) copy-start(s32[64]{0:T(128)} %param.11) | copy-start | bytes 772
  11.5 23.1 %copy-start.5 = (s32[64,14]{0,1:T(8,128)S(1)}, s32[64,14]{0,1:T(8,128)}, u32[]{:S(2)}) copy-start(s32[64,14]{0,1:T(8,128)} %param.10) | copy-start | bytes 10756
  11.5 23.3 %copy-start.1 = (s32[64]{0:T(128)S(1)}, s32[64]{0:T(128)}, u32[]{:S(2)}) copy-start(s32[64]{0:T(128)} %param.9) | copy-start | bytes 772
  12.7 23.8 %collective-permute-start = (bf16[128,512]{1,0:T(8,128)(2,1)S(1)}, bf16[128,512]{1,0:T(8,128)(2,1)S(1)}, u32[]{:S(2)}, u32[]{:S(2)}) collective-permute-start(bf16[128,512]{1,0:T(8,128)(2,1)S(1)} %multiply_convert_fusion), channel_id=1, source_target_pairs={{0,1},{1,2},{2,3},{3,4},{4,5},{5,6},{6,7},{7,0},{8,9},{9,10},{10,1... | collective-permute-start | bytes 393224 | tf_op jit(solution)/shard_map/ppermute | solution.py:17
  16.7 24.7 %collective-permute-start.1 = (bf16[128,512]{1,0:T(8,128)(2,1)S(1)}, bf16[128,512]{1,0:T(8,128)(2,1)S(1)}, u32[]{:S(2)}, u32[]{:S(2)}) collective-permute-start(bf16[128,512]{1,0:T(8,128)(2,1)S(1)} %multiply_convert_fusion), channel_id=1, source_target_pairs={{0,2},{1,3},{2,4},{3,5},{4,6},{5,7},{6,0},{7,1},{8,10},{9,11},{10,... | collective-permute-start | bytes 393224 | tf_op jit(solution)/shard_map/ppermute | solution.py:17
  20.9 23.5 %collective-permute-start.2 = (bf16[128,512]{1,0:T(8,128)(2,1)S(1)}, bf16[128,512]{1,0:T(8,128)(2,1)S(1)}, u32[]{:S(2)}, u32[]{:S(2)}) collective-permute-start(bf16[128,512]{1,0:T(8,128)(2,1)S(1)} %multiply_convert_fusion), channel_id=1, source_target_pairs={{0,3},{1,4},{2,5},{3,6},{4,7},{5,0},{6,1},{7,2},{8,11},{9,12},{10,... | collective-permute-start | bytes 393224 | tf_op jit(solution)/shard_map/ppermute | solution.py:17
  25.6 18.9 %collective-permute-start.3 = (bf16[128,512]{1,0:T(8,128)(2,1)S(1)}, bf16[128,512]{1,0:T(8,128)(2,1)S(1)}, u32[]{:S(2)}, u32[]{:S(2)}) collective-permute-start(bf16[128,512]{1,0:T(8,128)(2,1)S(1)} %multiply_convert_fusion), channel_id=1, source_target_pairs={{0,4},{1,5},{2,6},{3,7},{4,0},{5,1},{6,2},{7,3},{8,12},{9,13},{10,... | collective-permute-start | bytes 393224 | tf_op jit(solution)/shard_map/ppermute | solution.py:17
  29.1 15.8 %collective-permute-start.4 = (bf16[128,512]{1,0:T(8,128)(2,1)S(1)}, bf16[128,512]{1,0:T(8,128)(2,1)S(1)}, u32[]{:S(2)}, u32[]{:S(2)}) collective-permute-start(bf16[128,512]{1,0:T(8,128)(2,1)S(1)} %multiply_convert_fusion), channel_id=1, source_target_pairs={{0,5},{1,6},{2,7},{3,0},{4,1},{5,2},{6,3},{7,4},{8,13},{9,14},{10,... | collective-permute-start | bytes 393224 | tf_op jit(solution)/shard_map/ppermute | solution.py:17
  36.4 15.4 %collective-permute-start.5 = (bf16[128,512]{1,0:T(8,128)(2,1)S(1)}, bf16[128,512]{1,0:T(8,128)(2,1)S(1)}, u32[]{:S(2)}, u32[]{:S(2)}) collective-permute-start(bf16[128,512]{1,0:T(8,128)(2,1)S(1)} %multiply_convert_fusion), channel_id=1, source_target_pairs={{0,6},{1,7},{2,0},{3,1},{4,2},{5,3},{6,4},{7,5},{8,14},{9,15},{10,... | collective-permute-start | bytes 393224 | tf_op jit(solution)/shard_map/ppermute | solution.py:17
  41.4 13.8 %collective-permute-start.6 = (bf16[128,512]{1,0:T(8,128)(2,1)S(1)}, bf16[128,512]{1,0:T(8,128)(2,1)S(1)}, u32[]{:S(2)}, u32[]{:S(2)}) collective-permute-start(bf16[128,512]{1,0:T(8,128)(2,1)S(1)} %multiply_convert_fusion), channel_id=1, source_target_pairs={{0,7},{1,0},{2,1},{3,2},{4,3},{5,4},{6,5},{7,6},{8,15},{9,8},{10,9... | collective-permute-start | bytes 393224 | tf_op jit(solution)/shard_map/ppermute | solution.py:17
  111.2 1.2 copy-start.3
  111.2 1.2 copy-start.4
  114.9 20.6 %copy-start.2 = (f32[1024,16,128]{0,2,1:T(8,128)}, f32[1024,16,128]{0,2,1:T(8,128)S(1)}, u32[]{:S(2)}) copy-start(f32[1024,16,128]{0,2,1:T(8,128)S(1)} %get-tuple-element.13) | copy-start | bytes 25165828
  172.4 64.7 %all-to-all-start.1 = ((f32[64,16,512]{2,1,0:T(8,128)}), f32[64,16,512]{2,1,0:T(8,128)S(1)}, u32[]{:S(2)}, u32[]{:S(2)}) async-start(f32[64,16,512]{2,1,0:T(8,128)} %bitcast.77), calls=%async_computation.1 | async-start | bytes 4194304 | tf_op jit(solution)/shard_map/all_to_all | solution.py:24
  238.0 10.1 %all-to-all-start.2 = ((f32[8,1,1024]{2,1,0:T(1,128)}), f32[8,1,1024]{2,1,0:T(1,128)S(1)}, u32[]{:S(2)}, u32[]{:S(2)}) async-start(f32[8,1,1024]{2,1,0:T(1,128)} %reshape.265), calls=%async_computation.2 | async-start | bytes 65536 | tf_op jit(solution)/shard_map/all_to_all | solution.py:24
Sparse Core Ops, SparseCore 0:
  11.4 95.6 all-gather.4

commit v2 on v1

--- a/solution.py
+++ b/solution.py
@@ -55,7 +55,8 @@
     scores = jnp.where(usable[None, :, None], scores, FLOOR)
     row_top = jnp.max(scores, axis=(1, 2))
     row_total = jnp.sum(jnp.exp(scores - row_top[:, None, None]), axis=(1, 2))
-    stats = lax.all_gather(jnp.stack([row_top, row_total]), "grp", axis=0, tiled=False)
+    share = jnp.broadcast_to(jnp.stack([row_top, row_total])[None], (members, 2, row_top.shape[0]))
+    stats = lax.all_to_all(share, "grp", 0, 0, tiled=True)
     row_top = jnp.max(stats[:, 0], axis=0)
     row_total = jnp.sum(stats[:, 1] * jnp.exp(stats[:, 0] - row_top[None]), axis=0)
     logsum = row_top + jnp.log(row_total)
@@ -86,7 +87,8 @@
     weight_term = scale_down * lax.dot_general(
         tokens, grad_projected, contract, preferred_element_type=jnp.float32
     )
-    shard_rows = reduce_blocks(weight_term.reshape(groups, depth // groups, width), "dp")
+    row_blocks = weight_term.astype(jnp.bfloat16).reshape(groups, depth // groups, width)
+    shard_rows = reduce_blocks(row_blocks, "dp")
     columns = width // members
     by_member = jnp.swapaxes(shard_rows.reshape(depth // groups, members, columns), 0, 1)
     grad_w = reduce_blocks(by_member, "grp")

time: 258 us -> 231 us (0.90)
  blocking collectives: 46.2 us -> 28.7 us
  waiting for transfers between devices: 116 us -> 101 us
  matrix products: 10.8 us -> 13.7 us
    all_to_all x2, waiting for transfers between devices: 55 us -> 32.4 us  [reduce_blocks(): swapped = lax.all_to_all(blocks, axis, 0, 0, tiled=True)]
    all_gather x1 -> x0, blocking collectives: 19.3 us -> none  [on_device(): lax.all_gather(jnp.stack([row_top, row_total]), 'grp', axis=0, tiled=False)]
    all_to_all x0 -> x1, waiting for transfers between devices: none -> 7.23 us  [on_device(): stats = lax.all_to_all(share, 'grp', 0, 0, tiled=True)]
    all_to_all x0 -> x1, starting transfers between devices: none -> 6.46 us  [on_device(): stats = lax.all_to_all(share, 'grp', 0, 0, tiled=True)]
    all_to_all x2, starting transfers between devices: 16.8 us -> 12 us  [reduce_blocks(): swapped = lax.all_to_all(blocks, axis, 0, 0, tiled=True)]
    dot_general x1, matrix products: 2.38 us -> 5.76 us  [on_device(): jnp.einsum('rsc,sce->re', weights, caption_slots, preferred_element_type=...]
  transfers between devices with their start and end apart: 10 -> 11, of which waited for: 6 -> 7; matrix products, arithmetic and copies ran while one was open for 4% -> 5% of each run, Pallas kernels for 0% -> 0%
where the time goes in v2:
time: 231 us; the launch traced here: 230 us
  waiting for transfers between devices  101 us (44%)
  starting transfers between devices  47.7 us (21%)
  blocking collectives  28.7 us (12%)
  local copies, waits for them, and re-layouts  16.6 us (7%)
  between operations  15.1 us (7%)
  matrix products  13.7 us (6%)
  other arithmetic  7.35 us (3%)
    all_gather x1, waiting for transfers between devices, on_device(): every_block = lax.all_gather(captions, 'dp', axis=0, tiled=False)  50.5 us
    all_to_all x2, waiting for transfers between devices, reduce_blocks(): swapped = lax.all_to_all(blocks, axis, 0, 0, tiled=True)  32.4 us
    ppermute x7, starting transfers between devices, gather_ring(): received.append(lax.ppermute(part, axis, pairs))  29.2 us
    all_to_all x1, blocking collectives, reduce_blocks(): swapped = lax.all_to_all(blocks, axis, 0, 0, tiled=True)  28.7 us
    all_to_all x2, starting transfers between devices, reduce_blocks(): swapped = lax.all_to_all(blocks, axis, 0, 0, tiled=True)  12 us
    ppermute x7, waiting for transfers between devices, gather_ring(): received.append(lax.ppermute(part, axis, pairs))  10.4 us
    all_to_all x1, waiting for transfers between devices, on_device(): stats = lax.all_to_all(share, 'grp', 0, 0, tiled=True)  7.23 us
    all_to_all x1, starting transfers between devices, on_device(): stats = lax.all_to_all(share, 'grp', 0, 0, tiled=True)  6.46 us
  transfers between devices with their start and end apart: 11, of which 7 were waited for; matrix products, arithmetic and copies ran while one was open for 5% of the time, Pallas kernels for 0%

profile of v2, /device:TPU:1, one launch (start us, length us, event | category | flops | bytes accessed | tf_op | source)
XLA Modules:
  0.0 230.4 jit_solution(3864061351254422743)
XLA Ops:
  7.2 0.0 copy-start
  7.2 0.0 all-gather.3.cloned.1.call-start
  7.2 0.7 all-gather.3.cloned.1.call-update
  7.9 0.5 copy-done
  8.4 3.0 %multiply_multiply_fusion.2 = (f32[512,512]{1,0:T(8,128)S(1)}, f32[512,512]{1,0:T(8,128)}) fusion(bf16[512,1024]{1,0:T(8,128)(2,1)S(1)} %copy-done, bf16[1024,512]{1,0:T(8,128)(2,1)} %param.7), kind=kOutput, calls=%fused_computation.27 | convolution fusion | flops 538968064 | bytes 4194304 | tf_op jit(solution)/shard_map/dot_general | solution.py:39
  11.4 0.3 reshape.222
  11.7 0.6 reduce_sum.74
  12.3 0.1 multiply_reduce_fusion.1
  12.4 0.1 multiply_convert_fusion.1
  12.5 4.0 %collective-permute-start = (bf16[128,512]{1,0:T(8,128)(2,1)S(1)}, bf16[128,512]{1,0:T(8,128)(2,1)S(1)}, u32[]{:S(2)}, u32[]{:S(2)}) collective-permute-start(bf16[128,512]{1,0:T(8,128)(2,1)S(1)} %multiply_convert_fusion.1), channel_id=1, source_target_pairs={{0,1},{1,2},{2,3},{3,4},{4,5},{5,6},{6,7},{7,0},{8,9},{9,10},{10,1... | collective-permute-start | bytes 393224 | tf_op jit(solution)/shard_map/ppermute | solution.py:17
  16.6 4.2 %collective-permute-start.1 = (bf16[128,512]{1,0:T(8,128)(2,1)S(1)}, bf16[128,512]{1,0:T(8,128)(2,1)S(1)}, u32[]{:S(2)}, u32[]{:S(2)}) collective-permute-start(bf16[128,512]{1,0:T(8,128)(2,1)S(1)} %multiply_convert_fusion.1), channel_id=1, source_target_pairs={{0,2},{1,3},{2,4},{3,5},{4,6},{5,7},{6,0},{7,1},{8,10},{9,11},{10,... | collective-permute-start | bytes 393224 | tf_op jit(solution)/shard_map/ppermute | solution.py:17
  20.8 4.6 %collective-permute-start.2 = (bf16[128,512]{1,0:T(8,128)(2,1)S(1)}, bf16[128,512]{1,0:T(8,128)(2,1)S(1)}, u32[]{:S(2)}, u32[]{:S(2)}) collective-permute-start(bf16[128,512]{1,0:T(8,128)(2,1)S(1)} %multiply_convert_fusion.1), channel_id=1, source_target_pairs={{0,3},{1,4},{2,5},{3,6},{4,7},{5,0},{6,1},{7,2},{8,11},{9,12},{10,... | collective-permute-start | bytes 393224 | tf_op jit(solution)/shard_map/ppermute | solution.py:17
  25.5 3.5 %collective-permute-start.3 = (bf16[128,512]{1,0:T(8,128)(2,1)S(1)}, bf16[128,512]{1,0:T(8,128)(2,1)S(1)}, u32[]{:S(2)}, u32[]{:S(2)}) collective-permute-start(bf16[128,512]{1,0:T(8,128)(2,1)S(1)} %multiply_convert_fusion.1), channel_id=1, source_target_pairs={{0,4},{1,5},{2,6},{3,7},{4,0},{5,1},{6,2},{7,3},{8,12},{9,13},{10,... | collective-permute-start | bytes 393224 | tf_op jit(solution)/shard_map/ppermute | solution.py:17
  29.0 4.9 %collective-permute-start.4 = (bf16[128,512]{1,0:T(8,128)(2,1)S(1)}, bf16[128,512]{1,0:T(8,128)(2,1)S(1)}, u32[]{:S(2)}, u32[]{:S(2)}) collective-permute-start(bf16[128,512]{1,0:T(8,128)(2,1)S(1)} %multiply_convert_fusion.1), channel_id=1, source_target_pairs={{0,5},{1,6},{2,7},{3,0},{4,1},{5,2},{6,3},{7,4},{8,13},{9,14},{10,... | collective-permute-start | bytes 393224 | tf_op jit(solution)/shard_map/ppermute | solution.py:17
  33.9 0.6 dynamic_slice.17
  34.5 0.2 fusion.26
  34.7 0.7 gather_fusion.1
  36.1 0.1 broadcast_bitcast_fusion
  36.2 0.1 fusion.21
  36.3 0.0 collective-permute-done
  36.3 5.0 %collective-permute-start.5 = (bf16[128,512]{1,0:T(8,128)(2,1)S(1)}, bf16[128,512]{1,0:T(8,128)(2,1)S(1)}, u32[]{:S(2)}, u32[]{:S(2)}) collective-permute-start(bf16[128,512]{1,0:T(8,128)(2,1)S(1)} %multiply_convert_fusion.1), channel_id=1, source_target_pairs={{0,6},{1,7},{2,0},{3,1},{4,2},{5,3},{6,4},{7,5},{8,14},{9,15},{10,... | collective-permute-start | bytes 393224 | tf_op jit(solution)/shard_map/ppermute | solution.py:17
  41.3 3.0 %collective-permute-start.6 = (bf16[128,512]{1,0:T(8,128)(2,1)S(1)}, bf16[128,512]{1,0:T(8,128)(2,1)S(1)}, u32[]{:S(2)}, u32[]{:S(2)}) collective-permute-start(bf16[128,512]{1,0:T(8,128)(2,1)S(1)} %multiply_convert_fusion.1), channel_id=1, source_target_pairs={{0,7},{1,0},{2,1},{3,2},{4,3},{5,4},{6,5},{7,6},{8,15},{9,8},{10,9... | collective-permute-start | bytes 393224 | tf_op jit(solution)/shard_map/ppermute | solution.py:17
  44.4 0.5 collective-permute-done.4
  44.8 6.9 %collective-permute-done.5 = bf16[128,512]{1,0:T(8,128)(2,1)S(1)} collective-permute-done((bf16[128,512]{1,0:T(8,128)(2,1)S(1)}, bf16[128,512]{1,0:T(8,128)(2,1)S(1)}, u32[]{:S(2)}, u32[]{:S(2)}) %collective-permute-start.5) | collective-permute-done | bytes 131104 | tf_op jit(solution)/shard_map/ppermute | solution.py:17
  51.8 3.0 %collective-permute-done.6 = bf16[128,512]{1,0:T(8,128)(2,1)S(1)} collective-permute-done((bf16[128,512]{1,0:T(8,128)(2,1)S(1)}, bf16[128,512]{1,0:T(8,128)(2,1)S(1)}, u32[]{:S(2)}, u32[]{:S(2)}) %collective-permute-start.6) | collective-permute-done | bytes 131104 | tf_op jit(solution)/shard_map/ppermute | solution.py:17
  54.8 0.6 gather_fusion
  55.4 1.2 bitcast_select_fusion
  56.6 50.5 %all-gather.3.cloned.1.call-done = bf16[8192,512]{1,0:T(8,128)(2,1)} async-done(((bf16[128,512]{1,0:T(8,128)(2,1)}), bf16[8192,512]{1,0:T(8,128)(2,1)}) %all-gather.3.cloned.1.call-update) | async-done | bytes 8388624 | tf_op jit(solution)/shard_map/all_gather | solution.py:38
  107.1 4.1 %gather_fusion.2 = bf16[15,128,512]{2,1,0:T(8,128)(2,1)S(1)} fusion(bf16[64,128,512]{2,1,0:T(8,128)(2,1)} %bitcast.76, s32[1024]{0:T(1024)S(1)} %pad_clamp_fusion), kind=kCustom, calls=%fused_computation.2 | custom fusion | bytes 3932220 | tf_op jit(solution)/shard_map/jit(_take)/gather | solution.py:49
  111.2 0.0 copy-start.6
  111.2 0.3 broadcast_select_fusion
  111.5 1.0 copy-done.5
  112.4 0.1 copy-done.6
  112.5 2.5 %fusion.41 = (f32[1024]{0:T(1024)S(1)}, f32[1024,16,128]{0,2,1:T(8,128)S(1)}) fusion(bf16[15,128,512]{2,1,0:T(8,128)(2,1)S(1)} %broadcast_select_fusion, bf16[1,128,512]{2,1,0:T(8,128)(2,1)S(1)} %bitcast.78, bf16[1024,512]{1,0:T(8,128)(2,1)S(1)} %copy-done.5, pred[16]{0:T(512)(128)(4,1)S(1)} %iota_compare_fusion), kind=kOutput, calls=%fused_computation.100 | convolution fusion | flops 2157968384 | bytes 11538448 | tf_op jit(solution)/shard_map/re,sce->rsc/dot_general | solution.py:52
  115.1 1.2 exponential_reduce_fusion
  116.2 2.3 %copy-done.2 = f32[1024,16,128]{0,2,1:T(8,128)} copy-done((f32[1024,16,128]{0,2,1:T(8,128)}, f32[1024,16,128]{0,2,1:T(8,128)S(1)}, u32[]{:S(2)}) %copy-start.2) | copy-done | bytes 8388632
  118.6 0.6 broadcast_in_dim.72
  119.2 6.5 %all-to-all-start = ((f32[8,2,1024]{2,1,0:T(2,128)}), f32[8,2,1024]{2,1,0:T(2,128)S(1)}, u32[]{:S(2)}, u32[]{:S(2)}) async-start(f32[8,2,1024]{2,1,0:T(2,128)} %broadcast_in_dim.72), calls=%async_computation | async-start | bytes 131072 | tf_op jit(solution)/shard_map/all_to_all | solution.py:59
  125.7 7.2 %all-to-all-done = f32[8,2,1024]{2,1,0:T(2,128)S(1)} async-done(((f32[8,2,1024]{2,1,0:T(2,128)}), f32[8,2,1024]{2,1,0:T(2,128)S(1)}, u32[]{:S(2)}, u32[]{:S(2)}) %all-to-all-start) | async-done | bytes 65568 | tf_op jit(solution)/shard_map/all_to_all | solution.py:59
  132.9 0.1 fusion.40
  133.0 5.8 %fusion.2 = f32[1024,512]{1,0:T(8,128)S(1)} fusion(f32[1024,16,128]{0,2,1:T(8,128)} %copy-done.2, f32[1024]{0:T(1024)S(1)} %log_add_fusion, bf16[15,128,512]{2,1,0:T(8,128)(2,1)S(1)} %copy-done.4, bf16[1,128,512]{2,1,0:T(8,128)(2,1)S(1)} %bitcast.79), kind=kOutput, calls=%fused_computation.14 | convolution fusion | flops 2152726528 | bytes 12587008 | tf_op jit(solution)/shard_map/rsc,sce->re/dot_general | solution.py:68
  138.8 0.1 convert_element_type.44
  139.0 28.7 %all_to_all.20 = bf16[8,128,512]{2,1,0:T(8,128)(2,1)S(1)} all-to-all(bf16[8,128,512]{2,1,0:T(8,128)(2,1)S(1)} %bitcast.75), channel_id=1, replica_groups=mesh['dp'=64,'grp'=8] {'grp'}, dimensions={0} | all-to-all | bytes 2097152 | tf_op jit(solution)/shard_map/all_to_all | solution.py:24
  167.7 0.1 convert_reduce_fusion.1
  167.8 0.2 multiply_reduce_fusion
  168.0 0.8 broadcast_multiply_fusion
  168.9 0.2 broadcast_in_dim.73
  169.0 0.4 reshape.224
  169.4 2.5 %fusion.3 = bf16[1024,512]{0,1:T(8,128)(2,1)S(1)} fusion(bf16[512,1024]{1,0:T(8,128)(2,1)S(1)} %copy-done, f32[512,512]{1,0:T(8,128)} %get-tuple-element.11, f32[512,512]{1,0:T(8,128)S(1)} %reshape.224), kind=kOutput, calls=%fused_computation.17 | convolution fusion | flops 543162368 | bytes 4194304 | tf_op jit(solution)/shard_map/dot_general | solution.py:87
  171.9 1.4 copy.26
  173.3 8.6 %all-to-all-start.2 = ((bf16[64,16,512]{2,1,0:T(8,128)(2,1)}), bf16[64,16,512]{2,1,0:T(8,128)(2,1)S(1)}, u32[]{:S(2)}, u32[]{:S(2)}) async-start(bf16[64,16,512]{2,1,0:T(8,128)(2,1)} %bitcast.27), calls=%async_computation.2 | async-start | bytes 2097152 | tf_op jit(solution)/shard_map/all_to_all | solution.py:24
  182.0 1.1 slice.27
  183.1 1.3 gather_fusion.3
  184.4 26.1 %all-to-all-done.2 = bf16[64,16,512]{2,1,0:T(8,128)(2,1)S(1)} async-done(((bf16[64,16,512]{2,1,0:T(8,128)(2,1)}), bf16[64,16,512]{2,1,0:T(8,128)(2,1)S(1)}, u32[]{:S(2)}, u32[]{:S(2)}) %all-to-all-start.2) | async-done | bytes 1048608 | tf_op jit(solution)/shard_map/all_to_all | solution.py:24
  210.5 0.2 convert_reduce_fusion
  210.7 0.1 reshape.226
  210.8 0.7 reshape.262
  211.5 3.3 %all-to-all-start.3 = ((f32[8,1,1024]{2,1,0:T(1,128)}), f32[8,1,1024]{2,1,0:T(1,128)S(1)}, u32[]{:S(2)}, u32[]{:S(2)}) async-start(f32[8,1,1024]{2,1,0:T(1,128)} %reshape.262), calls=%async_computation.3 | async-start | bytes 65536 | tf_op jit(solution)/shard_map/all_to_all | solution.py:24
  214.8 0.6 dynamic-slice_subtract_fusion
  215.4 6.2 %all-to-all-done.3 = f32[8,1,1024]{2,1,0:T(1,128)S(1)} async-done(((f32[8,1,1024]{2,1,0:T(1,128)}), f32[8,1,1024]{2,1,0:T(1,128)S(1)}, u32[]{:S(2)}, u32[]{:S(2)}) %all-to-all-start.3) | async-done | bytes 32800 | tf_op jit(solution)/shard_map/all_to_all | solution.py:24
  221.6 0.5 broadcast.322
  222.1 0.7 reduce.3
  222.9 0.1 reshape.263
  222.9 0.6 reduce_sum.82
  (40 shorter events, 0.3 us)
Async XLA Ops:
  7.2 1.2 copy-start
  7.2 99.9 %all-gather.3.cloned.1.call-start = ((), (), s32[]{:S(2)}) async-start(), calls=%async_computation.4 | async-start | bytes 8519680 | tf_op jit(solution)/shard_map/all_gather | solution.py:38
  11.4 22.5 %copy-start.8 = (s32[64]{0:T(128)S(1)}, s32[64]{0:T(128)}, u32[]{:S(2)}) copy-start(s32[64]{0:T(128)} %param.11) | copy-start | bytes 772
  11.4 23.1 %copy-start.7 = (s32[64,14]{0,1:T(8,128)S(1)}, s32[64,14]{0,1:T(8,128)}, u32[]{:S(2)}) copy-start(s32[64,14]{0,1:T(8,128)} %param.10) | copy-start | bytes 10756
  11.4 23.3 %copy-start.1 = (s32[64]{0:T(128)S(1)}, s32[64]{0:T(128)}, u32[]{:S(2)}) copy-start(s32[64]{0:T(128)} %param.9) | copy-start | bytes 772
  12.5 23.8 %collective-permute-start = (bf16[128,512]{1,0:T(8,128)(2,1)S(1)}, bf16[128,512]{1,0:T(8,128)(2,1)S(1)}, u32[]{:S(2)}, u32[]{:S(2)}) collective-permute-start(bf16[128,512]{1,0:T(8,128)(2,1)S(1)} %multiply_convert_fusion.1), channel_id=1, source_target_pairs={{0,1},{1,2},{2,3},{3,4},{4,5},{5,6},{6,7},{7,0},{8,9},{9,10},{10,1... | collective-permute-start | bytes 393224 | tf_op jit(solution)/shard_map/ppermute | solution.py:17
  16.6 24.7 %collective-permute-start.1 = (bf16[128,512]{1,0:T(8,128)(2,1)S(1)}, bf16[128,512]{1,0:T(8,128)(2,1)S(1)}, u32[]{:S(2)}, u32[]{:S(2)}) collective-permute-start(bf16[128,512]{1,0:T(8,128)(2,1)S(1)} %multiply_convert_fusion.1), channel_id=1, source_target_pairs={{0,2},{1,3},{2,4},{3,5},{4,6},{5,7},{6,0},{7,1},{8,10},{9,11},{10,... | collective-permute-start | bytes 393224 | tf_op jit(solution)/shard_map/ppermute | solution.py:17
  20.8 23.5 %collective-permute-start.2 = (bf16[128,512]{1,0:T(8,128)(2,1)S(1)}, bf16[128,512]{1,0:T(8,128)(2,1)S(1)}, u32[]{:S(2)}, u32[]{:S(2)}) collective-permute-start(bf16[128,512]{1,0:T(8,128)(2,1)S(1)} %multiply_convert_fusion.1), channel_id=1, source_target_pairs={{0,3},{1,4},{2,5},{3,6},{4,7},{5,0},{6,1},{7,2},{8,11},{9,12},{10,... | collective-permute-start | bytes 393224 | tf_op jit(solution)/shard_map/ppermute | solution.py:17
  25.5 18.9 %collective-permute-start.3 = (bf16[128,512]{1,0:T(8,128)(2,1)S(1)}, bf16[128,512]{1,0:T(8,128)(2,1)S(1)}, u32[]{:S(2)}, u32[]{:S(2)}) collective-permute-start(bf16[128,512]{1,0:T(8,128)(2,1)S(1)} %multiply_convert_fusion.1), channel_id=1, source_target_pairs={{0,4},{1,5},{2,6},{3,7},{4,0},{5,1},{6,2},{7,3},{8,12},{9,13},{10,... | collective-permute-start | bytes 393224 | tf_op jit(solution)/shard_map/ppermute | solution.py:17
  29.0 15.8 %collective-permute-start.4 = (bf16[128,512]{1,0:T(8,128)(2,1)S(1)}, bf16[128,512]{1,0:T(8,128)(2,1)S(1)}, u32[]{:S(2)}, u32[]{:S(2)}) collective-permute-start(bf16[128,512]{1,0:T(8,128)(2,1)S(1)} %multiply_convert_fusion.1), channel_id=1, source_target_pairs={{0,5},{1,6},{2,7},{3,0},{4,1},{5,2},{6,3},{7,4},{8,13},{9,14},{10,... | collective-permute-start | bytes 393224 | tf_op jit(solution)/shard_map/ppermute | solution.py:17
  36.3 15.4 %collective-permute-start.5 = (bf16[128,512]{1,0:T(8,128)(2,1)S(1)}, bf16[128,512]{1,0:T(8,128)(2,1)S(1)}, u32[]{:S(2)}, u32[]{:S(2)}) collective-permute-start(bf16[128,512]{1,0:T(8,128)(2,1)S(1)} %multiply_convert_fusion.1), channel_id=1, source_target_pairs={{0,6},{1,7},{2,0},{3,1},{4,2},{5,3},{6,4},{7,5},{8,14},{9,15},{10,... | collective-permute-start | bytes 393224 | tf_op jit(solution)/shard_map/ppermute | solution.py:17
  41.3 13.5 %collective-permute-start.6 = (bf16[128,512]{1,0:T(8,128)(2,1)S(1)}, bf16[128,512]{1,0:T(8,128)(2,1)S(1)}, u32[]{:S(2)}, u32[]{:S(2)}) collective-permute-start(bf16[128,512]{1,0:T(8,128)(2,1)S(1)} %multiply_convert_fusion.1), channel_id=1, source_target_pairs={{0,7},{1,0},{2,1},{3,2},{4,3},{5,4},{6,5},{7,6},{8,15},{9,8},{10,9... | collective-permute-start | bytes 393224 | tf_op jit(solution)/shard_map/ppermute | solution.py:17
  111.2 1.3 copy-start.5
  111.2 1.4 copy-start.6
  111.5 3.6 %copy-start.3 = (bf16[15,128,512]{2,1,0:T(8,128)(2,1)}, bf16[15,128,512]{2,1,0:T(8,128)(2,1)S(1)}, u32[]{:S(2)}) copy-start(bf16[15,128,512]{2,1,0:T(8,128)(2,1)S(1)} %broadcast_select_fusion) | copy-start | bytes 5898244
  115.1 3.5 %copy-start.2 = (f32[1024,16,128]{0,2,1:T(8,128)}, f32[1024,16,128]{0,2,1:T(8,128)S(1)}, u32[]{:S(2)}) copy-start(f32[1024,16,128]{0,2,1:T(8,128)S(1)} %get-tuple-element.13) | copy-start | bytes 25165828
  115.1 18.0 %copy-start.4 = (bf16[15,128,512]{2,1,0:T(8,128)(2,1)S(1)}, bf16[15,128,512]{2,1,0:T(8,128)(2,1)}, u32[]{:S(2)}) copy-start(bf16[15,128,512]{2,1,0:T(8,128)(2,1)} %copy-done.3) | copy-start | bytes 5898244
  119.2 13.7 %all-to-all-start = ((f32[8,2,1024]{2,1,0:T(2,128)}), f32[8,2,1024]{2,1,0:T(2,128)S(1)}, u32[]{:S(2)}, u32[]{:S(2)}) async-start(f32[8,2,1024]{2,1,0:T(2,128)} %broadcast_in_dim.72), calls=%async_computation | async-start | bytes 131072 | tf_op jit(solution)/shard_map/all_to_all | solution.py:59
  173.3 37.2 %all-to-all-start.2 = ((bf16[64,16,512]{2,1,0:T(8,128)(2,1)}), bf16[64,16,512]{2,1,0:T(8,128)(2,1)S(1)}, u32[]{:S(2)}, u32[]{:S(2)}) async-start(bf16[64,16,512]{2,1,0:T(8,128)(2,1)} %bitcast.27), calls=%async_computation.2 | async-start | bytes 2097152 | tf_op jit(solution)/shard_map/all_to_all | solution.py:24
  211.5 10.2 %all-to-all-start.3 = ((f32[8,1,1024]{2,1,0:T(1,128)}), f32[8,1,1024]{2,1,0:T(1,128)S(1)}, u32[]{:S(2)}, u32[]{:S(2)}) async-start(f32[8,1,1024]{2,1,0:T(1,128)} %reshape.262), calls=%async_computation.3 | async-start | bytes 65536 | tf_op jit(solution)/shard_map/all_to_all | solution.py:24
Sparse Core Ops, SparseCore 0:
  11.4 95.6 all-gather.2

commit v3 on v2

--- a/solution.py
+++ b/solution.py
@@ -6,6 +6,7 @@
 SCORE_SCALE = 2.0
 EPSILON = 1e-06
 FLOOR = -1e30
+DP = ("chip", "core")
 
 
 def gather_ring(part, axis):
@@ -27,15 +28,17 @@
 
 def on_device(tokens, weight, captions, block_owner, confusable, counts):
     members = lax.axis_size("grp")
-    groups = lax.axis_size("dp")
-    group_index = lax.axis_index("dp")
+    groups = lax.axis_size(DP)
+    group_index = lax.axis_index(DP)
     member_index = lax.axis_index("grp")
     block_rows = captions.shape[0]
     width = captions.shape[1]
     depth = tokens.shape[1]
     frames = tokens.shape[0] // block_rows
     factor = SCORE_SCALE / width**0.5
-    every_block = lax.all_gather(captions, "dp", axis=0, tiled=False)
+    cores = lax.axis_size("core")
+    core_index = lax.axis_index("core")
+    same_core = lax.all_gather(captions, "chip", axis=0, tiled=False)
     projected = jnp.dot(tokens, weight, preferred_element_type=jnp.float32)
     activated = jax.nn.gelu(projected)
     pooled = jnp.mean(activated.reshape(block_rows, frames, width), axis=1)
@@ -46,7 +49,12 @@
     listed = jnp.concatenate([jnp.arange(groups, dtype=jnp.int32)[:, None], confusable], axis=1)
     slot_count = listed.shape[1] + 1
     sources = block_owner[listed[group_index]]
-    fetched = jnp.take(every_block, sources, axis=0)
+    partner_sources = block_owner[listed[group_index + 1 - 2 * core_index]]
+    outgoing = jnp.take(same_core, partner_sources // cores, axis=0)
+    incoming = lax.ppermute(outgoing, "core", [(i, (i + 1) % cores) for i in range(cores)])
+    local = jnp.take(same_core, sources // cores, axis=0)
+    mine = (sources % cores == core_index)[:, None, None]
+    fetched = jnp.where(mine, local, incoming)
     caption_slots = jnp.concatenate([captions[None], fetched], axis=0)
     usable = jnp.arange(slot_count, dtype=jnp.int32) < 2 + counts[group_index]
     scores = factor * jnp.einsum(
@@ -88,7 +96,7 @@
         tokens, grad_projected, contract, preferred_element_type=jnp.float32
     )
     row_blocks = weight_term.astype(jnp.bfloat16).reshape(groups, depth // groups, width)
-    shard_rows = reduce_blocks(row_blocks, "dp")
+    shard_rows = reduce_blocks(row_blocks, DP)
     columns = width // members
     by_member = jnp.swapaxes(shard_rows.reshape(depth // groups, members, columns), 0, 1)
     grad_w = reduce_blocks(by_member, "grp")
@@ -96,8 +104,11 @@
 
 
 def solution(mesh):
-    in_specs = (P(("dp", "grp"), None), P(), P(("dp", "grp"), None), P(), P(), P())
-    out_specs = (P(("dp", "grp")), P(("dp", "grp"), None), P("dp", "grp"))
+    cores = 2
+    devices = mesh.devices.reshape(mesh.shape["dp"] // cores, cores, mesh.shape["grp"])
+    fine = jax.sharding.Mesh(devices, ("chip", "core", "grp"))
+    in_specs = (P(DP + ("grp",), None), P(), P(DP + ("grp",), None), P(), P(), P())
+    out_specs = (P(DP + ("grp",)), P(DP + ("grp",), None), P(DP, "grp"))
     return jax.shard_map(
-        on_device, mesh=mesh, in_specs=in_specs, out_specs=out_specs, check_vma=False
+        on_device, mesh=fine, in_specs=in_specs, out_specs=out_specs, check_vma=False
     )

time: 231 us -> 262 us (1.13)
  waiting for transfers between devices: 101 us -> 112 us
  local copies, waits for them, and re-layouts: 16.6 us -> 26.9 us
  other arithmetic: 7.35 us -> 13.6 us
  starting transfers between devices: 47.7 us -> 51.2 us
    all_gather x1, waiting for transfers between devices: 50.5 us -> 66.8 us  [on_device(): same_core = lax.all_gather(captions, 'chip', axis=0, tiled=False)]
    ppermute x0 -> x1, starting transfers between devices: none -> 6.07 us  [on_device(): lax.ppermute(outgoing, 'core', [(i, (i + 1) % cores) for i in range(cores)])]
    unnamed x26 -> x34, local copies, waits for them, and re-layouts: 4.73 us -> 10.3 us
    ppermute x7, waiting for transfers between devices: 10.4 us -> 5.12 us  [gather_ring(): received.append(lax.ppermute(part, axis, pairs))]
    select_n x2, other arithmetic: 0.26 us -> 4.2 us  [the longest x1 2.26 us: on_device(): outgoing = jnp.take(same_core, partner_sources // cores, axis=0)]
    gather x1 -> x3, local copies, waits for them, and re-layouts: 4.05 us -> 6.4 us  [the longest x1 2.87 us: on_device(): local = jnp.take(same_core, sources // cores, axis=0)]
  transfers between devices with their start and end apart: 11 -> 12, of which waited for: 7 -> 6; matrix products, arithmetic and copies ran while one was open for 5% -> 12% of each run, Pallas kernels for 0% -> 0%
where the time goes in v3:
time: 262 us; the launch traced here: 261 us
  waiting for transfers between devices  112 us (43%)
  starting transfers between devices  51.2 us (20%)
  blocking collectives  28.1 us (11%)
  local copies, waits for them, and re-layouts  26.9 us (10%)
  between operations  15.1 us (6%)
  matrix products  13.8 us (5%)
  other arithmetic  13.6 us (5%)
    all_gather x1, waiting for transfers between devices, on_device(): same_core = lax.all_gather(captions, 'chip', axis=0, tiled=False)  66.8 us
    all_to_all x2, waiting for transfers between devices, reduce_blocks(): swapped = lax.all_to_all(blocks, axis, 0, 0, tiled=True)  32.4 us
    all_to_all x1, blocking collectives, reduce_blocks(): swapped = lax.all_to_all(blocks, axis, 0, 0, tiled=True)  28.1 us
    ppermute x7, starting transfers between devices, gather_ring(): received.append(lax.ppermute(part, axis, pairs))  27.8 us
    all_to_all x2, starting transfers between devices, reduce_blocks(): swapped = lax.all_to_all(blocks, axis, 0, 0, tiled=True)  12.6 us
    unnamed x34, local copies, waits for them, and re-layouts  10.3 us
    all_to_all x1, waiting for transfers between devices, on_device(): stats = lax.all_to_all(share, 'grp', 0, 0, tiled=True)  7.24 us
    ppermute x1, starting transfers between devices, on_device(): lax.ppermute(outgoing, 'core', [(i, (i + 1) % cores) for i in range(cores)])  6.07 us
  transfers between devices with their start and end apart: 12, of which 6 were waited for; matrix products, arithmetic and copies ran while one was open for 12% of the time, Pallas kernels for 0%

profile of v3, /device:TPU:1, one launch (start us, length us, event | category | flops | bytes accessed | tf_op | source)
XLA Modules:
  0.0 260.9 jit_solution(15612809085249765961)
XLA Ops:
  7.2 0.7 all-gather.3.cloned.1.call-update
  7.9 0.5 copy-done
  8.4 3.0 %multiply_multiply_fusion.2 = (f32[512,512]{1,0:T(8,128)S(1)}, f32[512,512]{1,0:T(8,128)}) fusion(bf16[512,1024]{1,0:T(8,128)(2,1)S(1)} %copy-done, bf16[1024,512]{1,0:T(8,128)(2,1)} %param.9), kind=kOutput, calls=%fused_computation.30 | convolution fusion | flops 538968064 | bytes 4194304 | tf_op jit(solution)/shard_map/dot_general | solution.py:42
  11.4 0.3 reshape.251
  11.7 0.6 reduce_sum.74
  12.5 0.5 add_rsqrt_fusion
  13.1 4.0 %collective-permute-start = (bf16[128,512]{1,0:T(8,128)(2,1)S(1)}, bf16[128,512]{1,0:T(8,128)(2,1)}, u32[]{:S(2)}, u32[]{:S(2)}) collective-permute-start(bf16[128,512]{1,0:T(8,128)(2,1)S(1)} %multiply_convert_fusion.1), channel_id=1, source_target_pairs={{0,1},{1,2},{2,3},{3,4},{4,5},{5,6},{6,7},{7,0},{8,9},{9,10},{10,1... | collective-permute-start | bytes 393224 | tf_op jit(solution)/shard_map/ppermute | solution.py:18
  17.1 4.2 %collective-permute-start.1 = (bf16[128,512]{1,0:T(8,128)(2,1)S(1)}, bf16[128,512]{1,0:T(8,128)(2,1)}, u32[]{:S(2)}, u32[]{:S(2)}) collective-permute-start(bf16[128,512]{1,0:T(8,128)(2,1)S(1)} %multiply_convert_fusion.1), channel_id=1, source_target_pairs={{0,2},{1,3},{2,4},{3,5},{4,6},{5,7},{6,0},{7,1},{8,10},{9,11},{10,... | collective-permute-start | bytes 393224 | tf_op jit(solution)/shard_map/ppermute | solution.py:18
  21.4 4.6 %collective-permute-start.2 = (bf16[128,512]{1,0:T(8,128)(2,1)S(1)}, bf16[128,512]{1,0:T(8,128)(2,1)}, u32[]{:S(2)}, u32[]{:S(2)}) collective-permute-start(bf16[128,512]{1,0:T(8,128)(2,1)S(1)} %multiply_convert_fusion.1), channel_id=1, source_target_pairs={{0,3},{1,4},{2,5},{3,6},{4,7},{5,0},{6,1},{7,2},{8,11},{9,12},{10,... | collective-permute-start | bytes 393224 | tf_op jit(solution)/shard_map/ppermute | solution.py:18
  26.0 3.5 %collective-permute-start.3 = (bf16[128,512]{1,0:T(8,128)(2,1)S(1)}, bf16[128,512]{1,0:T(8,128)(2,1)S(1)}, u32[]{:S(2)}, u32[]{:S(2)}) collective-permute-start(bf16[128,512]{1,0:T(8,128)(2,1)S(1)} %multiply_convert_fusion.1), channel_id=1, source_target_pairs={{0,4},{1,5},{2,6},{3,7},{4,0},{5,1},{6,2},{7,3},{8,12},{9,13},{10,... | collective-permute-start | bytes 393224 | tf_op jit(solution)/shard_map/ppermute | solution.py:18
  29.6 0.2 fusion.29
  29.8 0.7 gather_fusion.2
  30.5 0.7 gather_fusion.1
  31.1 0.6 dynamic_slice.20
  32.4 0.5 compare_and_fusion
  33.0 0.6 compare_and_fusion.1
  33.6 0.6 broadcast_bitcast_fusion
  34.2 0.7 fusion.21
  34.9 66.8 %all-gather.3.cloned.1.call-done = bf16[4096,512]{1,0:T(8,128)(2,1)} async-done(((bf16[128,512]{1,0:T(8,128)(2,1)}), bf16[4096,512]{1,0:T(8,128)(2,1)}) %all-gather.3.cloned.1.call-update) | async-done | bytes 4194320 | tf_op jit(solution)/shard_map/all_gather | solution.py:41
  101.7 2.9 %gather_fusion.5 = bf16[15,128,512]{2,1,0:T(8,128)(2,1)S(1)} fusion(bf16[32,128,512]{2,1,0:T(8,128)(2,1)} %bitcast.76, s32[1024]{0:T(1024)S(1)} %pad_clamp_fusion), kind=kCustom, calls=%fused_computation.1.clone | custom fusion | bytes 3932220 | tf_op jit(solution)/shard_map/jit(_take)/gather | solution.py:53
  104.6 2.3 broadcast_select_fusion
  106.9 6.1 %collective-permute-start.7 = (bf16[15,128,512]{2,1,0:T(8,128)(2,1)}, bf16[15,128,512]{2,1,0:T(8,128)(2,1)}, u32[]{:S(2)}, u32[]{:S(2)}) collective-permute-start(bf16[15,128,512]{2,1,0:T(8,128)(2,1)} %broadcast_select_fusion), channel_id=1, source_target_pairs={{0,8},{8,0},{1,9},{9,1},{2,10},{10,2},{3,11},{11,3},{4,12},{12,4},... | collective-permute-start | bytes 5898248 | tf_op jit(solution)/shard_map/ppermute | solution.py:54
  113.0 6.2 %collective-permute-start.4 = (bf16[128,512]{1,0:T(8,128)(2,1)S(1)}, bf16[128,512]{1,0:T(8,128)(2,1)S(1)}, u32[]{:S(2)}, u32[]{:S(2)}) collective-permute-start(bf16[128,512]{1,0:T(8,128)(2,1)S(1)} %multiply_convert_fusion.1), channel_id=1, source_target_pairs={{0,5},{1,6},{2,7},{3,0},{4,1},{5,2},{6,3},{7,4},{8,13},{9,14},{10,... | collective-permute-start | bytes 393224 | tf_op jit(solution)/shard_map/ppermute | solution.py:18
  119.2 1.6 bitcast_dynamic-update-slice_fusion.6
  120.8 3.0 %collective-permute-start.5 = (bf16[128,512]{1,0:T(8,128)(2,1)S(1)}, bf16[128,512]{1,0:T(8,128)(2,1)S(1)}, u32[]{:S(2)}, u32[]{:S(2)}) collective-permute-start(bf16[128,512]{1,0:T(8,128)(2,1)S(1)} %multiply_convert_fusion.1), channel_id=1, source_target_pairs={{0,6},{1,7},{2,0},{3,1},{4,2},{5,3},{6,4},{7,5},{8,14},{9,15},{10,... | collective-permute-start | bytes 393224 | tf_op jit(solution)/shard_map/ppermute | solution.py:18
  123.8 1.6 bitcast_dynamic-update-slice_fusion.5
  125.4 2.2 collective-permute-start.6
  127.6 1.6 bitcast_dynamic-update-slice_fusion.4
  129.1 0.7 bitcast_dynamic-update-slice_fusion.3
  129.8 0.6 bitcast_dynamic-update-slice_fusion.2
  130.4 3.0 %collective-permute-done.5 = bf16[128,512]{1,0:T(8,128)(2,1)S(1)} collective-permute-done((bf16[128,512]{1,0:T(8,128)(2,1)S(1)}, bf16[128,512]{1,0:T(8,128)(2,1)S(1)}, u32[]{:S(2)}, u32[]{:S(2)}) %collective-permute-start.5) | collective-permute-done | bytes 131104 | tf_op jit(solution)/shard_map/ppermute | solution.py:18
  133.4 0.7 bitcast_dynamic-update-slice_fusion.1
  134.1 2.1 collective-permute-done.6
  136.2 0.7 bitcast_dynamic-update-slice_fusion
  136.9 1.8 gather_fusion
  138.7 1.2 bitcast_select_fusion
  139.9 2.9 %gather_fusion.4 = bf16[15,128,512]{2,1,0:T(8,128)(2,1)S(1)} fusion(bf16[32,128,512]{2,1,0:T(8,128)(2,1)} %bitcast.77, s32[1024]{0:T(1024)S(1)} %pad_clamp_fusion.2), kind=kCustom, calls=%fused_computation.clone | custom fusion | bytes 3932220 | tf_op jit(solution)/shard_map/jit(_take)/gather | solution.py:55
  142.8 1.9 select_select_fusion
  144.8 2.5 fusion.45
  147.4 1.2 exponential_reduce_fusion
  148.5 2.3 copy-done.2
  150.9 0.6 broadcast_in_dim.80
  151.5 4.7 %all-to-all-start = ((f32[8,2,1024]{2,1,0:T(2,128)}), f32[8,2,1024]{2,1,0:T(2,128)S(1)}, u32[]{:S(2)}, u32[]{:S(2)}) async-start(f32[8,2,1024]{2,1,0:T(2,128)} %broadcast_in_dim.80), calls=%async_computation | async-start | bytes 131072 | tf_op jit(solution)/shard_map/all_to_all | solution.py:67
  156.2 7.2 %all-to-all-done = f32[8,2,1024]{2,1,0:T(2,128)S(1)} async-done(((f32[8,2,1024]{2,1,0:T(2,128)}), f32[8,2,1024]{2,1,0:T(2,128)S(1)}, u32[]{:S(2)}, u32[]{:S(2)}) %all-to-all-start) | async-done | bytes 65568 | tf_op jit(solution)/shard_map/all_to_all | solution.py:67
  163.6 5.8 %fusion.2 = f32[1024,512]{1,0:T(8,128)S(1)} fusion(f32[1024,16,128]{0,2,1:T(8,128)} %copy-done.2, f32[1024]{0:T(1024)S(1)} %log_add_fusion, bf16[15,128,512]{2,1,0:T(8,128)(2,1)S(1)} %copy-done.4, bf16[1,128,512]{2,1,0:T(8,128)(2,1)S(1)} %bitcast.80), kind=kOutput, calls=%fused_computation.17 | convolution fusion | flops 2152726528 | bytes 12587008 | tf_op jit(solution)/shard_map/rsc,sce->re/dot_general | solution.py:76
  169.5 28.1 %all_to_all.20 = bf16[8,128,512]{2,1,0:T(8,128)(2,1)S(1)} all-to-all(bf16[8,128,512]{2,1,0:T(8,128)(2,1)S(1)} %bitcast.75), channel_id=1, replica_groups=mesh['chip'=32,'core'=2,'grp'=8] {'grp'}, dimensions={0} | all-to-all | bytes 2097152 | tf_op jit(solution)/shard_map/all_to_all | solution.py:25
  197.8 0.2 multiply_reduce_fusion
  198.0 0.8 broadcast_multiply_fusion
  198.8 0.2 broadcast_in_dim.81
  199.0 0.4 reshape.253
  199.4 2.5 fusion.3
  201.9 1.3 copy.26
  203.2 9.2 %all-to-all-start.2 = ((bf16[64,16,512]{2,1,0:T(8,128)(2,1)}), bf16[64,16,512]{2,1,0:T(8,128)(2,1)S(1)}, u32[]{:S(2)}, u32[]{:S(2)}) async-start(bf16[64,16,512]{2,1,0:T(8,128)(2,1)} %bitcast.26), calls=%async_computation.2 | async-start | bytes 2097152 | tf_op jit(solution)/shard_map/all_to_all | solution.py:25
  212.5 1.1 slice.31
  213.6 1.3 gather_fusion.3
  214.9 26.1 %all-to-all-done.2 = bf16[64,16,512]{2,1,0:T(8,128)(2,1)S(1)} async-done(((bf16[64,16,512]{2,1,0:T(8,128)(2,1)}), bf16[64,16,512]{2,1,0:T(8,128)(2,1)S(1)}, u32[]{:S(2)}, u32[]{:S(2)}) %all-to-all-start.2) | async-done | bytes 1048608 | tf_op jit(solution)/shard_map/all_to_all | solution.py:25
  241.0 0.2 convert_reduce_fusion
  241.3 0.7 reshape.314
  242.0 3.3 %all-to-all-start.3 = ((f32[8,1,1024]{2,1,0:T(1,128)}), f32[8,1,1024]{2,1,0:T(1,128)S(1)}, u32[]{:S(2)}, u32[]{:S(2)}) async-start(f32[8,1,1024]{2,1,0:T(1,128)} %reshape.314), calls=%async_computation.3 | async-start | bytes 65536 | tf_op jit(solution)/shard_map/all_to_all | solution.py:25
  245.4 0.6 dynamic-slice_subtract_fusion
  245.9 6.2 %all-to-all-done.3 = f32[8,1,1024]{2,1,0:T(1,128)S(1)} async-done(((f32[8,1,1024]{2,1,0:T(1,128)}), f32[8,1,1024]{2,1,0:T(1,128)S(1)}, u32[]{:S(2)}, u32[]{:S(2)}) %all-to-all-start.3) | async-done | bytes 32800 | tf_op jit(solution)/shard_map/all_to_all | solution.py:25
  252.2 0.5 broadcast.403
  252.7 0.7 reduce.5
  253.5 0.6 reduce_sum.82
  (55 shorter events, 1.0 us)
Async XLA Ops:
  7.2 1.2 copy-start
  7.2 94.6 %all-gather.3.cloned.1.call-start = ((), (), s32[]{:S(2)}) async-start(), calls=%async_computation.4 | async-start | bytes 4325376 | tf_op jit(solution)/shard_map/all_gather | solution.py:41
  11.4 18.2 %copy-start.7 = (s32[64,14]{0,1:T(8,128)S(1)}, s32[64,14]{0,1:T(8,128)}, u32[]{:S(2)}) copy-start(s32[64,14]{0,1:T(8,128)} %param.12) | copy-start | bytes 10756
  11.4 18.4 %copy-start.1 = (s32[64]{0:T(128)S(1)}, s32[64]{0:T(128)}, u32[]{:S(2)}) copy-start(s32[64]{0:T(128)} %param.11) | copy-start | bytes 772
  11.4 19.7 %copy-start.12 = (s32[64]{0:T(128)S(1)}, s32[64]{0:T(128)}, u32[]{:S(2)}) copy-start(s32[64]{0:T(128)} %param.13) | copy-start | bytes 772
  13.1 99.9 %collective-permute-start = (bf16[128,512]{1,0:T(8,128)(2,1)S(1)}, bf16[128,512]{1,0:T(8,128)(2,1)}, u32[]{:S(2)}, u32[]{:S(2)}) collective-permute-start(bf16[128,512]{1,0:T(8,128)(2,1)S(1)} %multiply_convert_fusion.1), channel_id=1, source_target_pairs={{0,1},{1,2},{2,3},{3,4},{4,5},{5,6},{6,7},{7,0},{8,9},{9,10},{10,1... | collective-permute-start | bytes 393224 | tf_op jit(solution)/shard_map/ppermute | solution.py:18
  17.1 103.6 %collective-permute-start.1 = (bf16[128,512]{1,0:T(8,128)(2,1)S(1)}, bf16[128,512]{1,0:T(8,128)(2,1)}, u32[]{:S(2)}, u32[]{:S(2)}) collective-permute-start(bf16[128,512]{1,0:T(8,128)(2,1)S(1)} %multiply_convert_fusion.1), channel_id=1, source_target_pairs={{0,2},{1,3},{2,4},{3,5},{4,6},{5,7},{6,0},{7,1},{8,10},{9,11},{10,... | collective-permute-start | bytes 393224 | tf_op jit(solution)/shard_map/ppermute | solution.py:18
  21.4 104.0 %collective-permute-start.2 = (bf16[128,512]{1,0:T(8,128)(2,1)S(1)}, bf16[128,512]{1,0:T(8,128)(2,1)}, u32[]{:S(2)}, u32[]{:S(2)}) collective-permute-start(bf16[128,512]{1,0:T(8,128)(2,1)S(1)} %multiply_convert_fusion.1), channel_id=1, source_target_pairs={{0,3},{1,4},{2,5},{3,6},{4,7},{5,0},{6,1},{7,2},{8,11},{9,12},{10,... | collective-permute-start | bytes 393224 | tf_op jit(solution)/shard_map/ppermute | solution.py:18
  26.0 103.1 %collective-permute-start.3 = (bf16[128,512]{1,0:T(8,128)(2,1)S(1)}, bf16[128,512]{1,0:T(8,128)(2,1)S(1)}, u32[]{:S(2)}, u32[]{:S(2)}) collective-permute-start(bf16[128,512]{1,0:T(8,128)(2,1)S(1)} %multiply_convert_fusion.1), channel_id=1, source_target_pairs={{0,4},{1,5},{2,6},{3,7},{4,0},{5,1},{6,2},{7,3},{8,12},{9,13},{10,... | collective-permute-start | bytes 393224 | tf_op jit(solution)/shard_map/ppermute | solution.py:18
  106.9 31.9 %copy-start.10 = (pred[1024]{0:T(1024)(128)(4,1)S(1)}, pred[1024]{0:T(1024)(128)(4,1)}, u32[]{:S(2)}) copy-start(pred[1024]{0:T(1024)(128)(4,1)} %broadcast_bitcast_fusion) | copy-start | bytes 3076
  106.9 35.9 %collective-permute-start.7 = (bf16[15,128,512]{2,1,0:T(8,128)(2,1)}, bf16[15,128,512]{2,1,0:T(8,128)(2,1)}, u32[]{:S(2)}, u32[]{:S(2)}) collective-permute-start(bf16[15,128,512]{2,1,0:T(8,128)(2,1)} %broadcast_select_fusion), channel_id=1, source_target_pairs={{0,8},{8,0},{1,9},{9,1},{2,10},{10,2},{3,11},{11,3},{4,12},{12,4},... | collective-permute-start | bytes 5898248 | tf_op jit(solution)/shard_map/ppermute | solution.py:54
  113.0 16.8 %collective-permute-start.4 = (bf16[128,512]{1,0:T(8,128)(2,1)S(1)}, bf16[128,512]{1,0:T(8,128)(2,1)S(1)}, u32[]{:S(2)}, u32[]{:S(2)}) collective-permute-start(bf16[128,512]{1,0:T(8,128)(2,1)S(1)} %multiply_convert_fusion.1), channel_id=1, source_target_pairs={{0,5},{1,6},{2,7},{3,0},{4,1},{5,2},{6,3},{7,4},{8,13},{9,14},{10,... | collective-permute-start | bytes 393224 | tf_op jit(solution)/shard_map/ppermute | solution.py:18
  120.8 12.6 %collective-permute-start.5 = (bf16[128,512]{1,0:T(8,128)(2,1)S(1)}, bf16[128,512]{1,0:T(8,128)(2,1)S(1)}, u32[]{:S(2)}, u32[]{:S(2)}) collective-permute-start(bf16[128,512]{1,0:T(8,128)(2,1)S(1)} %multiply_convert_fusion.1), channel_id=1, source_target_pairs={{0,6},{1,7},{2,0},{3,1},{4,2},{5,3},{6,4},{7,5},{8,14},{9,15},{10,... | collective-permute-start | bytes 393224 | tf_op jit(solution)/shard_map/ppermute | solution.py:18
  125.4 10.8 %collective-permute-start.6 = (bf16[128,512]{1,0:T(8,128)(2,1)S(1)}, bf16[128,512]{1,0:T(8,128)(2,1)S(1)}, u32[]{:S(2)}, u32[]{:S(2)}) collective-permute-start(bf16[128,512]{1,0:T(8,128)(2,1)S(1)} %multiply_convert_fusion.1), channel_id=1, source_target_pairs={{0,7},{1,0},{2,1},{3,2},{4,3},{5,4},{6,5},{7,6},{8,15},{9,8},{10,9... | collective-permute-start | bytes 393224 | tf_op jit(solution)/shard_map/ppermute | solution.py:18
  139.9 2.9 %copy-start.8 = (pred[15]{0:T(512)(128)(4,1)S(1)}, pred[15]{0:T(512)(128)(4,1)}, u32[]{:S(2)}) copy-start(pred[15]{0:T(512)(128)(4,1)} %get-tuple-element.8) | copy-start | bytes 49
  139.9 2.9 %copy-start.9 = (pred[15]{0:T(512)(128)(4,1)S(1)}, pred[15]{0:T(512)(128)(4,1)}, u32[]{:S(2)}) copy-start(pred[15]{0:T(512)(128)(4,1)} %get-tuple-element.17) | copy-start | bytes 49
  142.8 2.0 copy-start.5
  142.8 2.0 copy-start.6
  144.8 2.5 copy-start.3
  147.3 3.5 %copy-start.2 = (f32[1024,16,128]{0,2,1:T(8,128)}, f32[1024,16,128]{0,2,1:T(8,128)S(1)}, u32[]{:S(2)}) copy-start(f32[1024,16,128]{0,2,1:T(8,128)S(1)} %get-tuple-element.21) | copy-start | bytes 25165828
  147.4 16.2 %copy-start.4 = (bf16[15,128,512]{2,1,0:T(8,128)(2,1)S(1)}, bf16[15,128,512]{2,1,0:T(8,128)(2,1)}, u32[]{:S(2)}) copy-start(bf16[15,128,512]{2,1,0:T(8,128)(2,1)} %copy-done.3) | copy-start | bytes 5898244
  151.5 11.9 %all-to-all-start = ((f32[8,2,1024]{2,1,0:T(2,128)}), f32[8,2,1024]{2,1,0:T(2,128)S(1)}, u32[]{:S(2)}, u32[]{:S(2)}) async-start(f32[8,2,1024]{2,1,0:T(2,128)} %broadcast_in_dim.80), calls=%async_computation | async-start | bytes 131072 | tf_op jit(solution)/shard_map/all_to_all | solution.py:67
  169.5 28.5 %copy-start.11 = (f32[128]{0:T(128)S(1)}, f32[128]{0:T(128)}, u32[]{:S(2)}) copy-start(f32[128]{0:T(128)} %get-tuple-element.15) | copy-start | bytes 1540
  203.2 37.8 %all-to-all-start.2 = ((bf16[64,16,512]{2,1,0:T(8,128)(2,1)}), bf16[64,16,512]{2,1,0:T(8,128)(2,1)S(1)}, u32[]{:S(2)}, u32[]{:S(2)}) async-start(bf16[64,16,512]{2,1,0:T(8,128)(2,1)} %bitcast.26), calls=%async_computation.2 | async-start | bytes 2097152 | tf_op jit(solution)/shard_map/all_to_all | solution.py:25
  242.0 10.1 %all-to-all-start.3 = ((f32[8,1,1024]{2,1,0:T(1,128)}), f32[8,1,1024]{2,1,0:T(1,128)S(1)}, u32[]{:S(2)}, u32[]{:S(2)}) async-start(f32[8,1,1024]{2,1,0:T(1,128)} %reshape.314), calls=%async_computation.3 | async-start | bytes 65536 | tf_op jit(solution)/shard_map/all_to_all | solution.py:25
Sparse Core Ops, SparseCore 0:
  11.2 90.4 all-gather.2

commit v4 on v3

--- a/solution.py
+++ b/solution.py
@@ -6,7 +6,7 @@
 SCORE_SCALE = 2.0
 EPSILON = 1e-06
 FLOOR = -1e30
-DP = ("chip", "core")
+DP = ("x", "z", "core")
 
 
 def gather_ring(part, axis):
@@ -36,9 +36,10 @@
     depth = tokens.shape[1]
     frames = tokens.shape[0] // block_rows
     factor = SCORE_SCALE / width**0.5
-    cores = lax.axis_size("core")
-    core_index = lax.axis_index("core")
-    same_core = lax.all_gather(captions, "chip", axis=0, tiled=False)
+    along_z = lax.all_gather(captions, "z", axis=0, tiled=False)
+    along_x = lax.all_gather(along_z, "x", axis=0, tiled=False)
+    every_block = lax.all_gather(along_x, "core", axis=0, tiled=False)
+    every_block = every_block.reshape((-1,) + captions.shape)
     projected = jnp.dot(tokens, weight, preferred_element_type=jnp.float32)
     activated = jax.nn.gelu(projected)
     pooled = jnp.mean(activated.reshape(block_rows, frames, width), axis=1)
@@ -49,12 +50,11 @@
     listed = jnp.concatenate([jnp.arange(groups, dtype=jnp.int32)[:, None], confusable], axis=1)
     slot_count = listed.shape[1] + 1
     sources = block_owner[listed[group_index]]
-    partner_sources = block_owner[listed[group_index + 1 - 2 * core_index]]
-    outgoing = jnp.take(same_core, partner_sources // cores, axis=0)
-    incoming = lax.ppermute(outgoing, "core", [(i, (i + 1) % cores) for i in range(cores)])
-    local = jnp.take(same_core, sources // cores, axis=0)
-    mine = (sources % cores == core_index)[:, None, None]
-    fetched = jnp.where(mine, local, incoming)
+    cores = lax.axis_size("core")
+    zs = lax.axis_size("z")
+    xs = lax.axis_size("x")
+    place = (sources % cores) * (xs * zs) + (sources // (cores * zs)) * zs + (sources // cores) % zs
+    fetched = jnp.take(every_block, place, axis=0)
     caption_slots = jnp.concatenate([captions[None], fetched], axis=0)
     usable = jnp.arange(slot_count, dtype=jnp.int32) < 2 + counts[group_index]
     scores = factor * jnp.einsum(
@@ -104,9 +104,9 @@
 
 
 def solution(mesh):
-    cores = 2
-    devices = mesh.devices.reshape(mesh.shape["dp"] // cores, cores, mesh.shape["grp"])
-    fine = jax.sharding.Mesh(devices, ("chip", "core", "grp"))
+    cores, zs = 2, 8
+    shape = (mesh.shape["dp"] // (cores * zs), zs, cores, mesh.shape["grp"])
+    fine = jax.sharding.Mesh(mesh.devices.reshape(shape), DP + ("grp",))
     in_specs = (P(DP + ("grp",), None), P(), P(DP + ("grp",), None), P(), P(), P())
     out_specs = (P(DP + ("grp",)), P(DP + ("grp",), None), P(DP, "grp"))
     return jax.shard_map(

time: 262 us -> 284 us (1.084)
  waiting for transfers between devices: 112 us -> 154 us
  local copies, waits for them, and re-layouts: 26.9 us -> 17.3 us
  other arithmetic: 13.6 us -> 7.39 us
    all_gather x1 -> x3, waiting for transfers between devices: 66.8 us -> 104 us  [the longest x1 58.3 us: on_device(): along_x = lax.all_gather(along_z, 'x', axis=0, tiled=False)]
    ppermute x1 -> x0, starting transfers between devices: 6.07 us -> none  [on_device(): lax.ppermute(outgoing, 'core', [(i, (i + 1) % cores) for i in range(cores)])]
    ppermute x7, waiting for transfers between devices: 5.12 us -> 10.2 us  [gather_ring(): received.append(lax.ppermute(part, axis, pairs))]
    unnamed x34 -> x28, local copies, waits for them, and re-layouts: 10.3 us -> 5.45 us
    all_to_all x2, starting transfers between devices: 12.6 us -> 16.7 us  [reduce_blocks(): swapped = lax.all_to_all(blocks, axis, 0, 0, tiled=True)]
    select_n x2, other arithmetic: 4.2 us -> 0.27 us  [on_device(): fetched = jnp.take(every_block, place, axis=0)]
    gather x3 -> x1, local copies, waits for them, and re-layouts: 6.4 us -> 4.05 us  [on_device(): fetched = jnp.take(every_block, place, axis=0)]
  transfers between devices with their start and end apart: 12 -> 13, of which waited for: 6 -> 7; matrix products, arithmetic and copies ran while one was open for 12% -> 3% of each run, Pallas kernels for 0% -> 0%
where the time goes in v4:
time: 284 us; the launch traced here: 283 us
  waiting for transfers between devices  154 us (54%)
  starting transfers between devices  48.6 us (17%)
  blocking collectives  28.1 us (10%)
  local copies, waits for them, and re-layouts  17.3 us (6%)
  between operations  14.9 us (5%)
  matrix products  12.6 us (4%)
  other arithmetic  7.39 us (3%)
    all_gather x1, waiting for transfers between devices, on_device(): along_x = lax.all_gather(along_z, 'x', axis=0, tiled=False)  58.3 us
    all_gather x1, waiting for transfers between devices, on_device(): along_z = lax.all_gather(captions, 'z', axis=0, tiled=False)  45.3 us
    all_to_all x2, waiting for transfers between devices, reduce_blocks(): swapped = lax.all_to_all(blocks, axis, 0, 0, tiled=True)  32.4 us
    all_to_all x1, blocking collectives, reduce_blocks(): swapped = lax.all_to_all(blocks, axis, 0, 0, tiled=True)  28.1 us
    ppermute x7, starting transfers between devices, gather_ring(): received.append(lax.ppermute(part, axis, pairs))  28.1 us
    all_to_all x2, starting transfers between devices, reduce_blocks(): swapped = lax.all_to_all(blocks, axis, 0, 0, tiled=True)  16.7 us
    ppermute x7, waiting for transfers between devices, gather_ring(): received.append(lax.ppermute(part, axis, pairs))  10.2 us
    all_to_all x1, waiting for transfers between devices, on_device(): stats = lax.all_to_all(share, 'grp', 0, 0, tiled=True)  7.23 us
  transfers between devices with their start and end apart: 13, of which 7 were waited for; matrix products, arithmetic and copies ran while one was open for 3% of the time, Pallas kernels for 0%

profile of v4, /device:TPU:1, one launch (start us, length us, event | category | flops | bytes accessed | tf_op | source)
XLA Modules:
  0.0 283.0 jit_solution(13324243440342063450)
XLA Ops:
  7.2 0.0 all-gather.7.cloned.1.call-start
  7.2 0.7 all-gather.7.cloned.1.call-update
  7.9 0.0 all-gather.9.cloned.1.call-start
  8.0 45.3 %all-gather.7.cloned.1.call-done = bf16[1024,512]{1,0:T(8,128)(2,1)} async-done(((bf16[128,512]{1,0:T(8,128)(2,1)}), bf16[1024,512]{1,0:T(8,128)(2,1)}) %all-gather.7.cloned.1.call-update) | async-done | bytes 1048592 | tf_op jit(solution)/shard_map/all_gather | solution.py:39
  53.3 0.0 all-gather.11.cloned.1.call-start
  53.3 58.3 %all-gather.9.cloned.1.call-done = bf16[32,128,512]{2,1,0:T(8,128)(2,1)} async-done(((bf16[8,128,512]{2,1,0:T(8,128)(2,1)}), bf16[32,128,512]{2,1,0:T(8,128)(2,1)}) %all-gather.9.cloned.1.call-update) | async-done | bytes 4194320 | tf_op jit(solution)/shard_map/all_gather | solution.py:40
  111.6 0.0 all-gather.11.cloned.1.call-update
  111.6 1.2 copy-done.8
  112.8 1.8 multiply_multiply_fusion.2
  114.7 0.3 reshape.364
  115.0 0.6 reduce_sum.74
  115.6 0.1 multiply_reduce_fusion.1
  115.7 0.1 multiply_convert_fusion.1
  115.8 3.1 %collective-permute-start = (bf16[128,512]{1,0:T(8,128)(2,1)S(1)}, bf16[128,512]{1,0:T(8,128)(2,1)S(1)}, u32[]{:S(2)}, u32[]{:S(2)}) collective-permute-start(bf16[128,512]{1,0:T(8,128)(2,1)S(1)} %multiply_convert_fusion.1), channel_id=1, source_target_pairs={{0,1},{1,2},{2,3},{3,4},{4,5},{5,6},{6,7},{7,0},{8,9},{9,10},{10,1... | collective-permute-start | bytes 393224 | tf_op jit(solution)/shard_map/ppermute | solution.py:18
  119.0 4.0 %collective-permute-start.1 = (bf16[128,512]{1,0:T(8,128)(2,1)S(1)}, bf16[128,512]{1,0:T(8,128)(2,1)S(1)}, u32[]{:S(2)}, u32[]{:S(2)}) collective-permute-start(bf16[128,512]{1,0:T(8,128)(2,1)S(1)} %multiply_convert_fusion.1), channel_id=1, source_target_pairs={{0,2},{1,3},{2,4},{3,5},{4,6},{5,7},{6,0},{7,1},{8,10},{9,11},{10,... | collective-permute-start | bytes 393224 | tf_op jit(solution)/shard_map/ppermute | solution.py:18
  123.0 4.4 %collective-permute-start.2 = (bf16[128,512]{1,0:T(8,128)(2,1)S(1)}, bf16[128,512]{1,0:T(8,128)(2,1)S(1)}, u32[]{:S(2)}, u32[]{:S(2)}) collective-permute-start(bf16[128,512]{1,0:T(8,128)(2,1)S(1)} %multiply_convert_fusion.1), channel_id=1, source_target_pairs={{0,3},{1,4},{2,5},{3,6},{4,7},{5,0},{6,1},{7,2},{8,11},{9,12},{10,... | collective-permute-start | bytes 393224 | tf_op jit(solution)/shard_map/ppermute | solution.py:18
  127.4 3.9 %collective-permute-start.3 = (bf16[128,512]{1,0:T(8,128)(2,1)S(1)}, bf16[128,512]{1,0:T(8,128)(2,1)S(1)}, u32[]{:S(2)}, u32[]{:S(2)}) collective-permute-start(bf16[128,512]{1,0:T(8,128)(2,1)S(1)} %multiply_convert_fusion.1), channel_id=1, source_target_pairs={{0,4},{1,5},{2,6},{3,7},{4,0},{5,1},{6,2},{7,3},{8,12},{9,13},{10,... | collective-permute-start | bytes 393224 | tf_op jit(solution)/shard_map/ppermute | solution.py:18
  131.3 4.4 %collective-permute-start.4 = (bf16[128,512]{1,0:T(8,128)(2,1)S(1)}, bf16[128,512]{1,0:T(8,128)(2,1)S(1)}, u32[]{:S(2)}, u32[]{:S(2)}) collective-permute-start(bf16[128,512]{1,0:T(8,128)(2,1)S(1)} %multiply_convert_fusion.1), channel_id=1, source_target_pairs={{0,5},{1,6},{2,7},{3,0},{4,1},{5,2},{6,3},{7,4},{8,13},{9,14},{10,... | collective-permute-start | bytes 393224 | tf_op jit(solution)/shard_map/ppermute | solution.py:18
  135.7 0.6 dynamic_slice.17
  136.3 0.2 fusion.26
  136.5 0.7 gather_fusion.1
  138.0 0.1 broadcast_bitcast_fusion
  138.0 0.1 fusion.21
  138.2 5.2 %collective-permute-start.5 = (bf16[128,512]{1,0:T(8,128)(2,1)S(1)}, bf16[128,512]{1,0:T(8,128)(2,1)S(1)}, u32[]{:S(2)}, u32[]{:S(2)}) collective-permute-start(bf16[128,512]{1,0:T(8,128)(2,1)S(1)} %multiply_convert_fusion.1), channel_id=1, source_target_pairs={{0,6},{1,7},{2,0},{3,1},{4,2},{5,3},{6,4},{7,5},{8,14},{9,15},{10,... | collective-permute-start | bytes 393224 | tf_op jit(solution)/shard_map/ppermute | solution.py:18
  143.4 3.1 %collective-permute-start.6 = (bf16[128,512]{1,0:T(8,128)(2,1)S(1)}, bf16[128,512]{1,0:T(8,128)(2,1)S(1)}, u32[]{:S(2)}, u32[]{:S(2)}) collective-permute-start(bf16[128,512]{1,0:T(8,128)(2,1)S(1)} %multiply_convert_fusion.1), channel_id=1, source_target_pairs={{0,7},{1,0},{2,1},{3,2},{4,3},{5,4},{6,5},{7,6},{8,15},{9,8},{10,9... | collective-permute-start | bytes 393224 | tf_op jit(solution)/shard_map/ppermute | solution.py:18
  146.6 8.3 %collective-permute-done.5 = bf16[128,512]{1,0:T(8,128)(2,1)S(1)} collective-permute-done((bf16[128,512]{1,0:T(8,128)(2,1)S(1)}, bf16[128,512]{1,0:T(8,128)(2,1)S(1)}, u32[]{:S(2)}, u32[]{:S(2)}) %collective-permute-start.5) | collective-permute-done | bytes 131104 | tf_op jit(solution)/shard_map/ppermute | solution.py:18
  154.9 1.9 collective-permute-done.6
  156.8 0.6 gather_fusion
  157.4 1.2 bitcast_select_fusion
  158.6 4.1 %gather_fusion.2 = bf16[15,128,512]{2,1,0:T(8,128)(2,1)S(1)} fusion(bf16[64,128,512]{2,1,0:T(8,128)(2,1)} %bitcast.96, s32[1024]{0:T(1024)S(1)} %pad_clamp_fusion), kind=kCustom, calls=%fused_computation.2 | custom fusion | bytes 3932220 | tf_op jit(solution)/shard_map/jit(_take)/gather | solution.py:57
  162.6 0.3 broadcast_select_fusion
  162.9 1.0 copy-done.5
  163.9 0.1 copy-done.6
  164.0 2.5 fusion.49
  166.5 1.2 exponential_reduce_fusion
  167.7 2.3 copy-done.2
  170.0 0.6 broadcast_in_dim.72
  170.7 3.7 %all-to-all-start = ((f32[8,2,1024]{2,1,0:T(2,128)}), f32[8,2,1024]{2,1,0:T(2,128)S(1)}, u32[]{:S(2)}, u32[]{:S(2)}) async-start(f32[8,2,1024]{2,1,0:T(2,128)} %broadcast_in_dim.72), calls=%async_computation | async-start | bytes 131072 | tf_op jit(solution)/shard_map/all_to_all | solution.py:67
  174.4 7.2 %all-to-all-done = f32[8,2,1024]{2,1,0:T(2,128)S(1)} async-done(((f32[8,2,1024]{2,1,0:T(2,128)}), f32[8,2,1024]{2,1,0:T(2,128)S(1)}, u32[]{:S(2)}, u32[]{:S(2)}) %all-to-all-start) | async-done | bytes 65568 | tf_op jit(solution)/shard_map/all_to_all | solution.py:67
  181.6 0.1 fusion.48
  181.7 5.8 %fusion.2 = f32[1024,512]{1,0:T(8,128)S(1)} fusion(f32[1024,16,128]{0,2,1:T(8,128)} %copy-done.2, f32[1024]{0:T(1024)S(1)} %log_add_fusion, bf16[15,128,512]{2,1,0:T(8,128)(2,1)S(1)} %copy-done.4, bf16[1,128,512]{2,1,0:T(8,128)(2,1)S(1)} %bitcast.99), kind=kOutput, calls=%fused_computation.14 | convolution fusion | flops 2152726528 | bytes 12587008 | tf_op jit(solution)/shard_map/rsc,sce->re/dot_general | solution.py:76
  187.6 0.1 convert_element_type.44
  187.7 28.1 %all_to_all.20 = bf16[8,128,512]{2,1,0:T(8,128)(2,1)S(1)} all-to-all(bf16[8,128,512]{2,1,0:T(8,128)(2,1)S(1)} %bitcast.93), channel_id=1, replica_groups=mesh['x'=4,'z'=8,'core'=2,'grp'=8] {'grp'}, dimensions={0} | all-to-all | bytes 2097152 | tf_op jit(solution)/shard_map/all_to_all | solution.py:25
  215.8 0.1 convert_reduce_fusion.1
  216.0 0.2 multiply_reduce_fusion
  216.2 0.8 broadcast_multiply_fusion
  217.0 0.2 broadcast_in_dim.73
  217.2 0.4 reshape.367
  217.6 2.5 fusion.3
  220.1 1.4 copy.26
  221.4 13.4 %all-to-all-start.2 = ((bf16[64,16,512]{2,1,0:T(8,128)(2,1)}), bf16[64,16,512]{2,1,0:T(8,128)(2,1)S(1)}, u32[]{:S(2)}, u32[]{:S(2)}) async-start(bf16[64,16,512]{2,1,0:T(8,128)(2,1)} %bitcast.29), calls=%async_computation.2 | async-start | bytes 2097152 | tf_op jit(solution)/shard_map/all_to_all | solution.py:25
  234.9 1.1 slice.27
  236.0 1.3 gather_fusion.3
  237.3 26.1 %all-to-all-done.2 = bf16[64,16,512]{2,1,0:T(8,128)(2,1)S(1)} async-done(((bf16[64,16,512]{2,1,0:T(8,128)(2,1)}), bf16[64,16,512]{2,1,0:T(8,128)(2,1)S(1)}, u32[]{:S(2)}, u32[]{:S(2)}) %all-to-all-start.2) | async-done | bytes 1048608 | tf_op jit(solution)/shard_map/all_to_all | solution.py:25
  263.4 0.2 convert_reduce_fusion
  263.6 0.1 reshape.369
  263.7 0.7 reshape.408
  264.4 3.3 %all-to-all-start.3 = ((f32[8,1,1024]{2,1,0:T(1,128)}), f32[8,1,1024]{2,1,0:T(1,128)S(1)}, u32[]{:S(2)}, u32[]{:S(2)}) async-start(f32[8,1,1024]{2,1,0:T(1,128)} %reshape.408), calls=%async_computation.3 | async-start | bytes 65536 | tf_op jit(solution)/shard_map/all_to_all | solution.py:25
  267.7 0.6 dynamic-slice_subtract_fusion
  268.3 6.2 %all-to-all-done.3 = f32[8,1,1024]{2,1,0:T(1,128)S(1)} async-done(((f32[8,1,1024]{2,1,0:T(1,128)}), f32[8,1,1024]{2,1,0:T(1,128)S(1)}, u32[]{:S(2)}, u32[]{:S(2)}) %all-to-all-start.3) | async-done | bytes 32800 | tf_op jit(solution)/shard_map/all_to_all | solution.py:25
  274.5 0.5 broadcast.559
  275.0 0.7 reduce.3
  275.8 0.1 reshape.409
  275.8 0.6 reduce_sum.82
  (48 shorter events, 0.4 us)
Async XLA Ops:
  7.2 104.5 %copy-start = (bf16[512,1024]{1,0:T(8,128)(2,1)S(1)}, bf16[512,1024]{1,0:T(8,128)(2,1)}, u32[]{:S(2)}) copy-start(bf16[512,1024]{1,0:T(8,128)(2,1)} %param.6) | copy-start | bytes 3145732
  7.2 46.1 %all-gather.7.cloned.1.call-start = ((), (), s32[]{:S(2)}) async-start(), calls=%async_computation.4 | async-start | bytes 1179648 | tf_op jit(solution)/shard_map/all_gather | solution.py:39
  7.9 103.7 %all-gather.9.cloned.1.call-start = ((), (), s32[]{:S(2)}) async-start(), calls=%async_computation.5 | async-start | bytes 5242880 | tf_op jit(solution)/shard_map/all_gather | solution.py:40
  53.3 105.3 %all-gather.11.cloned.1.call-start = ((), (), s32[]{:S(2)}) async-start(), calls=%async_computation.6 | async-start | bytes 12582912 | tf_op jit(solution)/shard_map/all_gather | solution.py:41
  111.6 1.2 copy-start.8
  114.7 21.1 %copy-start.9 = (s32[64]{0:T(128)S(1)}, s32[64]{0:T(128)}, u32[]{:S(2)}) copy-start(s32[64]{0:T(128)} %param.11) | copy-start | bytes 772
  114.7 21.6 %copy-start.7 = (s32[64,14]{0,1:T(8,128)S(1)}, s32[64,14]{0,1:T(8,128)}, u32[]{:S(2)}) copy-start(s32[64,14]{0,1:T(8,128)} %param.10) | copy-start | bytes 10756
  114.7 21.9 %copy-start.1 = (s32[64]{0:T(128)S(1)}, s32[64]{0:T(128)}, u32[]{:S(2)}) copy-start(s32[64]{0:T(128)} %param.9) | copy-start | bytes 772
  115.8 22.3 %collective-permute-start = (bf16[128,512]{1,0:T(8,128)(2,1)S(1)}, bf16[128,512]{1,0:T(8,128)(2,1)S(1)}, u32[]{:S(2)}, u32[]{:S(2)}) collective-permute-start(bf16[128,512]{1,0:T(8,128)(2,1)S(1)} %multiply_convert_fusion.1), channel_id=1, source_target_pairs={{0,1},{1,2},{2,3},{3,4},{4,5},{5,6},{6,7},{7,0},{8,9},{9,10},{10,1... | collective-permute-start | bytes 393224 | tf_op jit(solution)/shard_map/ppermute | solution.py:18
  119.0 24.4 %collective-permute-start.1 = (bf16[128,512]{1,0:T(8,128)(2,1)S(1)}, bf16[128,512]{1,0:T(8,128)(2,1)S(1)}, u32[]{:S(2)}, u32[]{:S(2)}) collective-permute-start(bf16[128,512]{1,0:T(8,128)(2,1)S(1)} %multiply_convert_fusion.1), channel_id=1, source_target_pairs={{0,2},{1,3},{2,4},{3,5},{4,6},{5,7},{6,0},{7,1},{8,10},{9,11},{10,... | collective-permute-start | bytes 393224 | tf_op jit(solution)/shard_map/ppermute | solution.py:18
  123.0 23.5 %collective-permute-start.2 = (bf16[128,512]{1,0:T(8,128)(2,1)S(1)}, bf16[128,512]{1,0:T(8,128)(2,1)S(1)}, u32[]{:S(2)}, u32[]{:S(2)}) collective-permute-start(bf16[128,512]{1,0:T(8,128)(2,1)S(1)} %multiply_convert_fusion.1), channel_id=1, source_target_pairs={{0,3},{1,4},{2,5},{3,6},{4,7},{5,0},{6,1},{7,2},{8,11},{9,12},{10,... | collective-permute-start | bytes 393224 | tf_op jit(solution)/shard_map/ppermute | solution.py:18
  127.4 19.1 %collective-permute-start.3 = (bf16[128,512]{1,0:T(8,128)(2,1)S(1)}, bf16[128,512]{1,0:T(8,128)(2,1)S(1)}, u32[]{:S(2)}, u32[]{:S(2)}) collective-permute-start(bf16[128,512]{1,0:T(8,128)(2,1)S(1)} %multiply_convert_fusion.1), channel_id=1, source_target_pairs={{0,4},{1,5},{2,6},{3,7},{4,0},{5,1},{6,2},{7,3},{8,12},{9,13},{10,... | collective-permute-start | bytes 393224 | tf_op jit(solution)/shard_map/ppermute | solution.py:18
  131.3 15.2 %collective-permute-start.4 = (bf16[128,512]{1,0:T(8,128)(2,1)S(1)}, bf16[128,512]{1,0:T(8,128)(2,1)S(1)}, u32[]{:S(2)}, u32[]{:S(2)}) collective-permute-start(bf16[128,512]{1,0:T(8,128)(2,1)S(1)} %multiply_convert_fusion.1), channel_id=1, source_target_pairs={{0,5},{1,6},{2,7},{3,0},{4,1},{5,2},{6,3},{7,4},{8,13},{9,14},{10,... | collective-permute-start | bytes 393224 | tf_op jit(solution)/shard_map/ppermute | solution.py:18
  138.2 16.7 %collective-permute-start.5 = (bf16[128,512]{1,0:T(8,128)(2,1)S(1)}, bf16[128,512]{1,0:T(8,128)(2,1)S(1)}, u32[]{:S(2)}, u32[]{:S(2)}) collective-permute-start(bf16[128,512]{1,0:T(8,128)(2,1)S(1)} %multiply_convert_fusion.1), channel_id=1, source_target_pairs={{0,6},{1,7},{2,0},{3,1},{4,2},{5,3},{6,4},{7,5},{8,14},{9,15},{10,... | collective-permute-start | bytes 393224 | tf_op jit(solution)/shard_map/ppermute | solution.py:18
  143.4 13.4 %collective-permute-start.6 = (bf16[128,512]{1,0:T(8,128)(2,1)S(1)}, bf16[128,512]{1,0:T(8,128)(2,1)S(1)}, u32[]{:S(2)}, u32[]{:S(2)}) collective-permute-start(bf16[128,512]{1,0:T(8,128)(2,1)S(1)} %multiply_convert_fusion.1), channel_id=1, source_target_pairs={{0,7},{1,0},{2,1},{3,2},{4,3},{5,4},{6,5},{7,6},{8,15},{9,8},{10,9... | collective-permute-start | bytes 393224 | tf_op jit(solution)/shard_map/ppermute | solution.py:18
  162.6 1.3 copy-start.5
  162.6 1.4 copy-start.6
  162.9 3.6 %copy-start.3 = (bf16[15,128,512]{2,1,0:T(8,128)(2,1)}, bf16[15,128,512]{2,1,0:T(8,128)(2,1)S(1)}, u32[]{:S(2)}) copy-start(bf16[15,128,512]{2,1,0:T(8,128)(2,1)S(1)} %broadcast_select_fusion) | copy-start | bytes 5898244
  166.5 3.5 %copy-start.2 = (f32[1024,16,128]{0,2,1:T(8,128)}, f32[1024,16,128]{0,2,1:T(8,128)S(1)}, u32[]{:S(2)}) copy-start(f32[1024,16,128]{0,2,1:T(8,128)S(1)} %get-tuple-element.13) | copy-start | bytes 25165828
  166.5 15.2 %copy-start.4 = (bf16[15,128,512]{2,1,0:T(8,128)(2,1)S(1)}, bf16[15,128,512]{2,1,0:T(8,128)(2,1)}, u32[]{:S(2)}) copy-start(bf16[15,128,512]{2,1,0:T(8,128)(2,1)} %copy-done.3) | copy-start | bytes 5898244
  170.7 11.0 %all-to-all-start = ((f32[8,2,1024]{2,1,0:T(2,128)}), f32[8,2,1024]{2,1,0:T(2,128)S(1)}, u32[]{:S(2)}, u32[]{:S(2)}) async-start(f32[8,2,1024]{2,1,0:T(2,128)} %broadcast_in_dim.72), calls=%async_computation | async-start | bytes 131072 | tf_op jit(solution)/shard_map/all_to_all | solution.py:67
  221.4 42.0 %all-to-all-start.2 = ((bf16[64,16,512]{2,1,0:T(8,128)(2,1)}), bf16[64,16,512]{2,1,0:T(8,128)(2,1)S(1)}, u32[]{:S(2)}, u32[]{:S(2)}) async-start(bf16[64,16,512]{2,1,0:T(8,128)(2,1)} %bitcast.29), calls=%async_computation.2 | async-start | bytes 2097152 | tf_op jit(solution)/shard_map/all_to_all | solution.py:25
  264.4 10.1 %all-to-all-start.3 = ((f32[8,1,1024]{2,1,0:T(1,128)}), f32[8,1,1024]{2,1,0:T(1,128)S(1)}, u32[]{:S(2)}, u32[]{:S(2)}) async-start(f32[8,1,1024]{2,1,0:T(1,128)} %reshape.408), calls=%async_computation.3 | async-start | bytes 65536 | tf_op jit(solution)/shard_map/all_to_all | solution.py:25
Sparse Core Ops, SparseCore 0:
  10.1 43.0 all-gather.6
  55.3 56.2 all-gather.8
  113.7 29.8 all-gather.10

commit v5 on v2

--- a/solution.py
+++ b/solution.py
@@ -87,11 +87,16 @@
     weight_term = scale_down * lax.dot_general(
         tokens, grad_projected, contract, preferred_element_type=jnp.float32
     )
-    row_blocks = weight_term.astype(jnp.bfloat16).reshape(groups, depth // groups, width)
-    shard_rows = reduce_blocks(row_blocks, "dp")
-    columns = width // members
-    by_member = jnp.swapaxes(shard_rows.reshape(depth // groups, members, columns), 0, 1)
-    grad_w = reduce_blocks(by_member, "grp")
+    rows = depth // groups
+    half = width // members // 2
+    quarters = weight_term.astype(jnp.bfloat16).reshape(depth, members, 2, half)
+    dp_first = quarters[:, :, 0].reshape(groups, rows, members * half)
+    grp_first = jnp.swapaxes(quarters[:, :, 1], 0, 1)
+    dp_rows = reduce_blocks(dp_first, "dp")
+    grp_columns = reduce_blocks(grp_first, "grp")
+    left = reduce_blocks(jnp.swapaxes(dp_rows.reshape(rows, members, half), 0, 1), "grp")
+    right = reduce_blocks(grp_columns.reshape(groups, rows, half), "dp")
+    grad_w = jnp.concatenate([left, right], axis=1)
     return (clip_loss, grad_pooled, grad_w)
 
 

time: 231 us -> 262 us (1.13)
  blocking collectives: 28.7 us -> 54.6 us
  local copies, waits for them, and re-layouts: 16.6 us -> 22.3 us
  waiting for transfers between devices: 101 us -> 97.3 us
    all_to_all x1 -> x2, blocking collectives: 28.7 us -> 54.6 us  [reduce_blocks(): swapped = lax.all_to_all(blocks, axis, 0, 0, tiled=True)]
    all_to_all x2 -> x3, waiting for transfers between devices: 32.4 us -> 28.5 us  [reduce_blocks(): swapped = lax.all_to_all(blocks, axis, 0, 0, tiled=True)]
    unnamed x26 -> x29, local copies, waits for them, and re-layouts: 4.73 us -> 8.32 us
    all_to_all x2 -> x3, starting transfers between devices: 12 us -> 14.1 us  [reduce_blocks(): swapped = lax.all_to_all(blocks, axis, 0, 0, tiled=True)]
  transfers between devices with their start and end apart: 11 -> 12, of which waited for: 7 -> 8; matrix products, arithmetic and copies ran while one was open for 5% -> 5% of each run, Pallas kernels for 0% -> 0%
where the time goes in v5:
time: 262 us; the launch traced here: 261 us
  waiting for transfers between devices  97.3 us (37%)
  blocking collectives  54.6 us (21%)
  starting transfers between devices  49.8 us (19%)
  local copies, waits for them, and re-layouts  22.3 us (9%)
  between operations  15.2 us (6%)
  matrix products  13.7 us (5%)
  other arithmetic  8.43 us (3%)
    all_to_all x2, blocking collectives, reduce_blocks(): swapped = lax.all_to_all(blocks, axis, 0, 0, tiled=True)  54.6 us
    all_gather x1, waiting for transfers between devices, on_device(): every_block = lax.all_gather(captions, 'dp', axis=0, tiled=False)  50.5 us
    ppermute x7, starting transfers between devices, gather_ring(): received.append(lax.ppermute(part, axis, pairs))  29.2 us
    all_to_all x3, waiting for transfers between devices, reduce_blocks(): swapped = lax.all_to_all(blocks, axis, 0, 0, tiled=True)  28.5 us
    all_to_all x3, starting transfers between devices, reduce_blocks(): swapped = lax.all_to_all(blocks, axis, 0, 0, tiled=True)  14.1 us
    ppermute x7, waiting for transfers between devices, gather_ring(): received.append(lax.ppermute(part, axis, pairs))  10.4 us
    unnamed x29, local copies, waits for them, and re-layouts  8.32 us
    all_to_all x1, waiting for transfers between devices, on_device(): stats = lax.all_to_all(share, 'grp', 0, 0, tiled=True)  7.23 us
  transfers between devices with their start and end apart: 12, of which 8 were waited for; matrix products, arithmetic and copies ran while one was open for 5% of the time, Pallas kernels for 0%

profile of v5, /device:TPU:1, one launch (start us, length us, event | category | flops | bytes accessed | tf_op | source)
XLA Modules:
  0.0 261.4 jit_solution(3744027230131031125)
XLA Ops:
  7.2 0.7 all-gather.3.cloned.1.call-update
  7.9 0.5 copy-done
  8.4 3.0 %multiply_multiply_fusion.2 = (f32[512,512]{1,0:T(8,128)S(1)}, f32[512,512]{1,0:T(8,128)}) fusion(bf16[512,1024]{1,0:T(8,128)(2,1)S(1)} %copy-done, bf16[1024,512]{1,0:T(8,128)(2,1)} %param.7), kind=kOutput, calls=%fused_computation.27 | convolution fusion | flops 538968064 | bytes 4194304 | tf_op jit(solution)/shard_map/dot_general | solution.py:39
  11.4 0.3 reshape.225
  11.7 0.6 reduce_sum.92
  12.3 0.1 multiply_reduce_fusion.1
  12.4 0.1 multiply_convert_fusion.1
  12.5 4.0 %collective-permute-start = (bf16[128,512]{1,0:T(8,128)(2,1)S(1)}, bf16[128,512]{1,0:T(8,128)(2,1)S(1)}, u32[]{:S(2)}, u32[]{:S(2)}) collective-permute-start(bf16[128,512]{1,0:T(8,128)(2,1)S(1)} %multiply_convert_fusion.1), channel_id=1, source_target_pairs={{0,1},{1,2},{2,3},{3,4},{4,5},{5,6},{6,7},{7,0},{8,9},{9,10},{10,1... | collective-permute-start | bytes 393224 | tf_op jit(solution)/shard_map/ppermute | solution.py:17
  16.6 4.2 %collective-permute-start.1 = (bf16[128,512]{1,0:T(8,128)(2,1)S(1)}, bf16[128,512]{1,0:T(8,128)(2,1)S(1)}, u32[]{:S(2)}, u32[]{:S(2)}) collective-permute-start(bf16[128,512]{1,0:T(8,128)(2,1)S(1)} %multiply_convert_fusion.1), channel_id=1, source_target_pairs={{0,2},{1,3},{2,4},{3,5},{4,6},{5,7},{6,0},{7,1},{8,10},{9,11},{10,... | collective-permute-start | bytes 393224 | tf_op jit(solution)/shard_map/ppermute | solution.py:17
  20.8 4.6 %collective-permute-start.2 = (bf16[128,512]{1,0:T(8,128)(2,1)S(1)}, bf16[128,512]{1,0:T(8,128)(2,1)S(1)}, u32[]{:S(2)}, u32[]{:S(2)}) collective-permute-start(bf16[128,512]{1,0:T(8,128)(2,1)S(1)} %multiply_convert_fusion.1), channel_id=1, source_target_pairs={{0,3},{1,4},{2,5},{3,6},{4,7},{5,0},{6,1},{7,2},{8,11},{9,12},{10,... | collective-permute-start | bytes 393224 | tf_op jit(solution)/shard_map/ppermute | solution.py:17
  25.5 3.5 %collective-permute-start.3 = (bf16[128,512]{1,0:T(8,128)(2,1)S(1)}, bf16[128,512]{1,0:T(8,128)(2,1)S(1)}, u32[]{:S(2)}, u32[]{:S(2)}) collective-permute-start(bf16[128,512]{1,0:T(8,128)(2,1)S(1)} %multiply_convert_fusion.1), channel_id=1, source_target_pairs={{0,4},{1,5},{2,6},{3,7},{4,0},{5,1},{6,2},{7,3},{8,12},{9,13},{10,... | collective-permute-start | bytes 393224 | tf_op jit(solution)/shard_map/ppermute | solution.py:17
  29.0 4.9 %collective-permute-start.4 = (bf16[128,512]{1,0:T(8,128)(2,1)S(1)}, bf16[128,512]{1,0:T(8,128)(2,1)S(1)}, u32[]{:S(2)}, u32[]{:S(2)}) collective-permute-start(bf16[128,512]{1,0:T(8,128)(2,1)S(1)} %multiply_convert_fusion.1), channel_id=1, source_target_pairs={{0,5},{1,6},{2,7},{3,0},{4,1},{5,2},{6,3},{7,4},{8,13},{9,14},{10,... | collective-permute-start | bytes 393224 | tf_op jit(solution)/shard_map/ppermute | solution.py:17
  33.9 0.6 dynamic_slice.17
  34.5 0.2 fusion.25
  34.7 0.7 gather_fusion.1
  36.3 5.0 %collective-permute-start.5 = (bf16[128,512]{1,0:T(8,128)(2,1)S(1)}, bf16[128,512]{1,0:T(8,128)(2,1)S(1)}, u32[]{:S(2)}, u32[]{:S(2)}) collective-permute-start(bf16[128,512]{1,0:T(8,128)(2,1)S(1)} %multiply_convert_fusion.1), channel_id=1, source_target_pairs={{0,6},{1,7},{2,0},{3,1},{4,2},{5,3},{6,4},{7,5},{8,14},{9,15},{10,... | collective-permute-start | bytes 393224 | tf_op jit(solution)/shard_map/ppermute | solution.py:17
  41.3 3.0 %collective-permute-start.6 = (bf16[128,512]{1,0:T(8,128)(2,1)S(1)}, bf16[128,512]{1,0:T(8,128)(2,1)S(1)}, u32[]{:S(2)}, u32[]{:S(2)}) collective-permute-start(bf16[128,512]{1,0:T(8,128)(2,1)S(1)} %multiply_convert_fusion.1), channel_id=1, source_target_pairs={{0,7},{1,0},{2,1},{3,2},{4,3},{5,4},{6,5},{7,6},{8,15},{9,8},{10,9... | collective-permute-start | bytes 393224 | tf_op jit(solution)/shard_map/ppermute | solution.py:17
  44.4 0.5 collective-permute-done.4
  44.8 6.9 %collective-permute-done.5 = bf16[128,512]{1,0:T(8,128)(2,1)S(1)} collective-permute-done((bf16[128,512]{1,0:T(8,128)(2,1)S(1)}, bf16[128,512]{1,0:T(8,128)(2,1)S(1)}, u32[]{:S(2)}, u32[]{:S(2)}) %collective-permute-start.5) | collective-permute-done | bytes 131104 | tf_op jit(solution)/shard_map/ppermute | solution.py:17
  51.8 3.0 %collective-permute-done.6 = bf16[128,512]{1,0:T(8,128)(2,1)S(1)} collective-permute-done((bf16[128,512]{1,0:T(8,128)(2,1)S(1)}, bf16[128,512]{1,0:T(8,128)(2,1)S(1)}, u32[]{:S(2)}, u32[]{:S(2)}) %collective-permute-start.6) | collective-permute-done | bytes 131104 | tf_op jit(solution)/shard_map/ppermute | solution.py:17
  54.8 0.6 gather_fusion
  55.4 1.2 bitcast_select_fusion
  56.6 50.5 %all-gather.3.cloned.1.call-done = bf16[8192,512]{1,0:T(8,128)(2,1)} async-done(((bf16[128,512]{1,0:T(8,128)(2,1)}), bf16[8192,512]{1,0:T(8,128)(2,1)}) %all-gather.3.cloned.1.call-update) | async-done | bytes 8388624 | tf_op jit(solution)/shard_map/all_gather | solution.py:38
  107.1 4.1 %gather_fusion.2 = bf16[15,128,512]{2,1,0:T(8,128)(2,1)S(1)} fusion(bf16[64,128,512]{2,1,0:T(8,128)(2,1)} %bitcast.89, s32[1024]{0:T(1024)S(1)} %pad_clamp_fusion), kind=kCustom, calls=%fused_computation.2 | custom fusion | bytes 3932220 | tf_op jit(solution)/shard_map/jit(_take)/gather | solution.py:49
  111.2 0.3 broadcast_select_fusion
  111.5 1.0 copy-done.5
  112.4 0.1 copy-done.6
  112.5 2.5 fusion.41
  115.1 1.2 exponential_reduce_fusion
  116.2 2.3 copy-done.2
  118.6 0.6 broadcast_in_dim.72
  119.2 6.5 %all-to-all-start = ((f32[8,2,1024]{2,1,0:T(2,128)}), f32[8,2,1024]{2,1,0:T(2,128)S(1)}, u32[]{:S(2)}, u32[]{:S(2)}) async-start(f32[8,2,1024]{2,1,0:T(2,128)} %broadcast_in_dim.72), calls=%async_computation | async-start | bytes 131072 | tf_op jit(solution)/shard_map/all_to_all | solution.py:59
  125.7 7.2 %all-to-all-done = f32[8,2,1024]{2,1,0:T(2,128)S(1)} async-done(((f32[8,2,1024]{2,1,0:T(2,128)}), f32[8,2,1024]{2,1,0:T(2,128)S(1)}, u32[]{:S(2)}, u32[]{:S(2)}) %all-to-all-start) | async-done | bytes 65568 | tf_op jit(solution)/shard_map/all_to_all | solution.py:59
  133.0 5.8 %fusion.2 = f32[1024,512]{1,0:T(8,128)S(1)} fusion(f32[1024,16,128]{0,2,1:T(8,128)} %copy-done.2, f32[1024]{0:T(1024)S(1)} %log_add_fusion, bf16[15,128,512]{2,1,0:T(8,128)(2,1)S(1)} %copy-done.4, bf16[1,128,512]{2,1,0:T(8,128)(2,1)S(1)} %bitcast.92), kind=kOutput, calls=%fused_computation.13 | convolution fusion | flops 2152726528 | bytes 12587008 | tf_op jit(solution)/shard_map/rsc,sce->re/dot_general | solution.py:68
  138.8 0.1 convert_element_type.47
  139.0 28.7 %all_to_all.30 = bf16[8,128,512]{2,1,0:T(8,128)(2,1)S(1)} all-to-all(bf16[8,128,512]{2,1,0:T(8,128)(2,1)S(1)} %bitcast.86), channel_id=1, replica_groups=mesh['dp'=64,'grp'=8] {'grp'}, dimensions={0} | all-to-all | bytes 2097152 | tf_op jit(solution)/shard_map/all_to_all | solution.py:24
  167.7 0.1 convert_reduce_fusion
  167.8 0.2 multiply_reduce_fusion
  168.0 0.8 broadcast_multiply_fusion
  168.9 0.2 broadcast_in_dim.73
  169.0 0.4 reshape.227
  169.4 2.5 multiply_convert_fusion
  171.9 1.2 fusion.39
  173.1 2.5 copy.38
  175.6 2.2 reshape_squeeze.3
  177.8 26.0 %all_to_all.31 = bf16[64,16,256]{2,1,0:T(8,128)(2,1)S(1)} all-to-all(bf16[64,16,256]{2,1,0:T(8,128)(2,1)} %reshape_squeeze.3), channel_id=1, replica_groups=mesh['dp'=64,'grp'=8] {'dp'}, dimensions={0} | all-to-all | bytes 1048576 | tf_op jit(solution)/shard_map/all_to_all | solution.py:24
  203.7 3.5 %all-to-all-start.4 = ((bf16[8,1024,32]{1,2,0:T(8,128)(2,1)}), bf16[8,1024,32]{1,2,0:T(8,128)(2,1)S(1)}, u32[]{:S(2)}, u32[]{:S(2)}) async-start(bf16[8,1024,32]{1,2,0:T(8,128)(2,1)} %get-tuple-element.6), calls=%async_computation.4 | async-start | bytes 1048576 | tf_op jit(solution)/shard_map/all_to_all | solution.py:24
  207.3 1.1 slice.35
  208.3 0.1 convert_reduce_fusion.2
  208.5 0.7 reshape.268
  209.2 15.9 %all-to-all-done.4 = bf16[8,1024,32]{1,2,0:T(8,128)(2,1)S(1)} async-done(((bf16[8,1024,32]{1,2,0:T(8,128)(2,1)}), bf16[8,1024,32]{1,2,0:T(8,128)(2,1)S(1)}, u32[]{:S(2)}, u32[]{:S(2)}) %all-to-all-start.4) | async-done | bytes 524320 | tf_op jit(solution)/shard_map/all_to_all | solution.py:24
  225.2 3.3 %all-to-all-start.3 = ((f32[8,1,512]{2,1,0:T(1,128)}), f32[8,1,512]{2,1,0:T(1,128)S(1)}, u32[]{:S(2)}, u32[]{:S(2)}) async-start(f32[8,1,512]{2,1,0:T(1,128)} %reshape.268), calls=%async_computation.3 | async-start | bytes 32768 | tf_op jit(solution)/shard_map/all_to_all | solution.py:24
  228.6 0.2 copy.34
  228.8 0.9 reshape.266
  229.7 5.4 %all-to-all-done.3 = f32[8,1,512]{2,1,0:T(1,128)S(1)} async-done(((f32[8,1,512]{2,1,0:T(1,128)}), f32[8,1,512]{2,1,0:T(1,128)S(1)}, u32[]{:S(2)}, u32[]{:S(2)}) %all-to-all-start.3) | async-done | bytes 16416 | tf_op jit(solution)/shard_map/all_to_all | solution.py:24
  235.1 7.2 %all-to-all-start.5 = ((f32[64,1,512]{2,1,0:T(1,128)}), f32[64,1,512]{2,1,0:T(1,128)S(1)}, u32[]{:S(2)}, u32[]{:S(2)}) async-start(f32[64,1,512]{2,1,0:T(1,128)} %reshape.266), calls=%async_computation.5 | async-start | bytes 262144 | tf_op jit(solution)/shard_map/all_to_all | solution.py:24
  242.3 1.3 gather_fusion.3
  243.6 0.6 dynamic-slice_subtract_fusion
  244.2 0.5 broadcast.322
  244.7 0.7 reduce.4
  245.5 7.2 %all-to-all-done.5 = f32[64,1,512]{2,1,0:T(1,128)S(1)} async-done(((f32[64,1,512]{2,1,0:T(1,128)}), f32[64,1,512]{2,1,0:T(1,128)S(1)}, u32[]{:S(2)}, u32[]{:S(2)}) %all-to-all-start.5) | async-done | bytes 131104 | tf_op jit(solution)/shard_map/all_to_all | solution.py:24
  252.7 1.0 reduce.3
  253.6 0.2 reshape.267
  253.9 0.7 pad_maximum_fusion.4
  (52 shorter events, 0.9 us)
Async XLA Ops:
  7.2 1.2 copy-start
  7.2 99.9 %all-gather.3.cloned.1.call-start = ((), (), s32[]{:S(2)}) async-start(), calls=%async_computation.6 | async-start | bytes 8519680 | tf_op jit(solution)/shard_map/all_gather | solution.py:38
  11.4 22.5 %copy-start.8 = (s32[64]{0:T(128)S(1)}, s32[64]{0:T(128)}, u32[]{:S(2)}) copy-start(s32[64]{0:T(128)} %param.11) | copy-start | bytes 772
  11.4 23.1 %copy-start.7 = (s32[64,14]{0,1:T(8,128)S(1)}, s32[64,14]{0,1:T(8,128)}, u32[]{:S(2)}) copy-start(s32[64,14]{0,1:T(8,128)} %param.10) | copy-start | bytes 10756
  11.4 23.3 %copy-start.1 = (s32[64]{0:T(128)S(1)}, s32[64]{0:T(128)}, u32[]{:S(2)}) copy-start(s32[64]{0:T(128)} %param.9) | copy-start | bytes 772
  12.5 23.8 %collective-permute-start = (bf16[128,512]{1,0:T(8,128)(2,1)S(1)}, bf16[128,512]{1,0:T(8,128)(2,1)S(1)}, u32[]{:S(2)}, u32[]{:S(2)}) collective-permute-start(bf16[128,512]{1,0:T(8,128)(2,1)S(1)} %multiply_convert_fusion.1), channel_id=1, source_target_pairs={{0,1},{1,2},{2,3},{3,4},{4,5},{5,6},{6,7},{7,0},{8,9},{9,10},{10,1... | collective-permute-start | bytes 393224 | tf_op jit(solution)/shard_map/ppermute | solution.py:17
  16.6 24.7 %collective-permute-start.1 = (bf16[128,512]{1,0:T(8,128)(2,1)S(1)}, bf16[128,512]{1,0:T(8,128)(2,1)S(1)}, u32[]{:S(2)}, u32[]{:S(2)}) collective-permute-start(bf16[128,512]{1,0:T(8,128)(2,1)S(1)} %multiply_convert_fusion.1), channel_id=1, source_target_pairs={{0,2},{1,3},{2,4},{3,5},{4,6},{5,7},{6,0},{7,1},{8,10},{9,11},{10,... | collective-permute-start | bytes 393224 | tf_op jit(solution)/shard_map/ppermute | solution.py:17
  20.8 23.5 %collective-permute-start.2 = (bf16[128,512]{1,0:T(8,128)(2,1)S(1)}, bf16[128,512]{1,0:T(8,128)(2,1)S(1)}, u32[]{:S(2)}, u32[]{:S(2)}) collective-permute-start(bf16[128,512]{1,0:T(8,128)(2,1)S(1)} %multiply_convert_fusion.1), channel_id=1, source_target_pairs={{0,3},{1,4},{2,5},{3,6},{4,7},{5,0},{6,1},{7,2},{8,11},{9,12},{10,... | collective-permute-start | bytes 393224 | tf_op jit(solution)/shard_map/ppermute | solution.py:17
  25.5 18.9 %collective-permute-start.3 = (bf16[128,512]{1,0:T(8,128)(2,1)S(1)}, bf16[128,512]{1,0:T(8,128)(2,1)S(1)}, u32[]{:S(2)}, u32[]{:S(2)}) collective-permute-start(bf16[128,512]{1,0:T(8,128)(2,1)S(1)} %multiply_convert_fusion.1), channel_id=1, source_target_pairs={{0,4},{1,5},{2,6},{3,7},{4,0},{5,1},{6,2},{7,3},{8,12},{9,13},{10,... | collective-permute-start | bytes 393224 | tf_op jit(solution)/shard_map/ppermute | solution.py:17
  29.0 15.8 %collective-permute-start.4 = (bf16[128,512]{1,0:T(8,128)(2,1)S(1)}, bf16[128,512]{1,0:T(8,128)(2,1)S(1)}, u32[]{:S(2)}, u32[]{:S(2)}) collective-permute-start(bf16[128,512]{1,0:T(8,128)(2,1)S(1)} %multiply_convert_fusion.1), channel_id=1, source_target_pairs={{0,5},{1,6},{2,7},{3,0},{4,1},{5,2},{6,3},{7,4},{8,13},{9,14},{10,... | collective-permute-start | bytes 393224 | tf_op jit(solution)/shard_map/ppermute | solution.py:17
  36.3 15.4 %collective-permute-start.5 = (bf16[128,512]{1,0:T(8,128)(2,1)S(1)}, bf16[128,512]{1,0:T(8,128)(2,1)S(1)}, u32[]{:S(2)}, u32[]{:S(2)}) collective-permute-start(bf16[128,512]{1,0:T(8,128)(2,1)S(1)} %multiply_convert_fusion.1), channel_id=1, source_target_pairs={{0,6},{1,7},{2,0},{3,1},{4,2},{5,3},{6,4},{7,5},{8,14},{9,15},{10,... | collective-permute-start | bytes 393224 | tf_op jit(solution)/shard_map/ppermute | solution.py:17
  41.3 13.5 %collective-permute-start.6 = (bf16[128,512]{1,0:T(8,128)(2,1)S(1)}, bf16[128,512]{1,0:T(8,128)(2,1)S(1)}, u32[]{:S(2)}, u32[]{:S(2)}) collective-permute-start(bf16[128,512]{1,0:T(8,128)(2,1)S(1)} %multiply_convert_fusion.1), channel_id=1, source_target_pairs={{0,7},{1,0},{2,1},{3,2},{4,3},{5,4},{6,5},{7,6},{8,15},{9,8},{10,9... | collective-permute-start | bytes 393224 | tf_op jit(solution)/shard_map/ppermute | solution.py:17
  111.2 1.3 copy-start.5
  111.2 1.4 copy-start.6
  111.5 3.6 %copy-start.3 = (bf16[15,128,512]{2,1,0:T(8,128)(2,1)}, bf16[15,128,512]{2,1,0:T(8,128)(2,1)S(1)}, u32[]{:S(2)}) copy-start(bf16[15,128,512]{2,1,0:T(8,128)(2,1)S(1)} %broadcast_select_fusion) | copy-start | bytes 5898244
  115.1 3.5 %copy-start.2 = (f32[1024,16,128]{0,2,1:T(8,128)}, f32[1024,16,128]{0,2,1:T(8,128)S(1)}, u32[]{:S(2)}) copy-start(f32[1024,16,128]{0,2,1:T(8,128)S(1)} %get-tuple-element.15) | copy-start | bytes 25165828
  115.1 18.0 %copy-start.4 = (bf16[15,128,512]{2,1,0:T(8,128)(2,1)S(1)}, bf16[15,128,512]{2,1,0:T(8,128)(2,1)}, u32[]{:S(2)}) copy-start(bf16[15,128,512]{2,1,0:T(8,128)(2,1)} %copy-done.3) | copy-start | bytes 5898244
  119.2 13.7 %all-to-all-start = ((f32[8,2,1024]{2,1,0:T(2,128)}), f32[8,2,1024]{2,1,0:T(2,128)S(1)}, u32[]{:S(2)}, u32[]{:S(2)}) async-start(f32[8,2,1024]{2,1,0:T(2,128)} %broadcast_in_dim.72), calls=%async_computation | async-start | bytes 131072 | tf_op jit(solution)/shard_map/all_to_all | solution.py:59
  203.7 21.4 %all-to-all-start.4 = ((bf16[8,1024,32]{1,2,0:T(8,128)(2,1)}), bf16[8,1024,32]{1,2,0:T(8,128)(2,1)S(1)}, u32[]{:S(2)}, u32[]{:S(2)}) async-start(bf16[8,1024,32]{1,2,0:T(8,128)(2,1)} %get-tuple-element.6), calls=%async_computation.4 | async-start | bytes 1048576 | tf_op jit(solution)/shard_map/all_to_all | solution.py:24
  225.2 9.9 %all-to-all-start.3 = ((f32[8,1,512]{2,1,0:T(1,128)}), f32[8,1,512]{2,1,0:T(1,128)S(1)}, u32[]{:S(2)}, u32[]{:S(2)}) async-start(f32[8,1,512]{2,1,0:T(1,128)} %reshape.268), calls=%async_computation.3 | async-start | bytes 32768 | tf_op jit(solution)/shard_map/all_to_all | solution.py:24
  235.1 17.6 %all-to-all-start.5 = ((f32[64,1,512]{2,1,0:T(1,128)}), f32[64,1,512]{2,1,0:T(1,128)S(1)}, u32[]{:S(2)}, u32[]{:S(2)}) async-start(f32[64,1,512]{2,1,0:T(1,128)} %reshape.266), calls=%async_computation.5 | async-start | bytes 262144 | tf_op jit(solution)/shard_map/all_to_all | solution.py:24
Sparse Core Ops, SparseCore 0:
  11.4 95.6 all-gather.2

commit v6 on v2

--- a/solution.py
+++ b/solution.py
@@ -46,34 +46,43 @@
     listed = jnp.concatenate([jnp.arange(groups, dtype=jnp.int32)[:, None], confusable], axis=1)
     slot_count = listed.shape[1] + 1
     sources = block_owner[listed[group_index]]
-    fetched = jnp.take(every_block, sources, axis=0)
-    caption_slots = jnp.concatenate([captions[None], fetched], axis=0)
+    slot_sources = jnp.concatenate([group_index[None].astype(sources.dtype), sources])
+    caption_slots = jnp.take(every_block, slot_sources, axis=0)
     usable = jnp.arange(slot_count, dtype=jnp.int32) < 2 + counts[group_index]
     scores = factor * jnp.einsum(
         "re,sce->rsc", group_clips, caption_slots, preferred_element_type=jnp.float32
     )
     scores = jnp.where(usable[None, :, None], scores, FLOOR)
     row_top = jnp.max(scores, axis=(1, 2))
-    row_total = jnp.sum(jnp.exp(scores - row_top[:, None, None]), axis=(1, 2))
-    share = jnp.broadcast_to(jnp.stack([row_top, row_total])[None], (members, 2, row_top.shape[0]))
-    stats = lax.all_to_all(share, "grp", 0, 0, tiled=True)
-    row_top = jnp.max(stats[:, 0], axis=0)
-    row_total = jnp.sum(stats[:, 1] * jnp.exp(stats[:, 0] - row_top[None]), axis=0)
-    logsum = row_top + jnp.log(row_total)
+    raised = jnp.exp(scores - row_top[:, None, None])
+    row_total = jnp.sum(raised, axis=(1, 2))
+    partial_sums = jnp.einsum(
+        "rsc,sce->re", raised.astype(jnp.bfloat16), caption_slots, preferred_element_type=jnp.float32
+    )
+    slot = (jnp.arange(members) == member_index)[:, None, None]
+    placed = jnp.where(slot, jnp.stack([row_top, row_total])[None], 0.0)
+    every_stat = lax.psum(placed, "grp")
+    blocks = partial_sums.astype(jnp.bfloat16).reshape(members, block_rows, width)
+    received = lax.all_to_all(blocks, "grp", 0, 0, tiled=True)
     own_start = member_index * block_rows
+    got = lax.dynamic_slice_in_dim(every_stat, own_start, block_rows, 2)
+    tops = got[:, 0]
+    totals = got[:, 1]
+    top = jnp.max(tops, axis=0)
+    total = jnp.sum(totals * jnp.exp(tops - top[None]), axis=0)
+    logsum = top + jnp.log(total)
+    share = jnp.exp(tops - logsum[None])
     own_scores = lax.dynamic_slice_in_dim(scores[:, 1, :], own_start, block_rows, 0)
     positive = jnp.diagonal(own_scores)
-    clip_loss = lax.dynamic_slice_in_dim(logsum, own_start, block_rows, 0) - positive
-    weights = jnp.exp(scores - logsum[:, None, None]).astype(jnp.bfloat16)
-    partial_sums = jnp.einsum(
-        "rsc,sce->re", weights, caption_slots, preferred_element_type=jnp.float32
-    )
-    own_rows = lax.dynamic_slice_in_dim(partial_sums, own_start, block_rows, 0) - caption_slots[
-        1
-    ].astype(jnp.float32)
-    partial_sums = lax.dynamic_update_slice_in_dim(partial_sums, own_rows, own_start, 0)
-    parts = partial_sums.astype(jnp.bfloat16).reshape(members, block_rows, width)
-    grad_unit = factor * reduce_blocks(parts, "grp")
+    clip_loss = logsum - positive
+    parts = received.astype(jnp.float32) * share[:, :, None]
+    own_partial = lax.dynamic_slice_in_dim(partial_sums, own_start, block_rows, 0)
+    own_share = lax.dynamic_index_in_dim(share, member_index, 0, keepdims=False)
+    own_part = own_partial * own_share[:, None] - caption_slots[1].astype(jnp.float32)
+    own_part = own_part.astype(jnp.bfloat16).astype(jnp.float32)
+    mine = (jnp.arange(members) == member_index)[:, None, None]
+    parts = jnp.where(mine, own_part[None], parts)
+    grad_unit = factor * jnp.sum(parts, axis=0)
     grad_pooled = inverse_rms * (
         grad_unit - unit_rows * jnp.mean(grad_unit * unit_rows, axis=-1, keepdims=True)
     )

time: 231 us -> 275 us (1.19)
  waiting for transfers between devices: 101 us -> 129 us
  blocking collectives: 28.7 us -> 54.8 us
  starting transfers between devices: 47.7 us -> 36 us
  other arithmetic: 7.35 us -> 14.7 us
  local copies, waits for them, and re-layouts: 16.6 us -> 12.1 us
    psum x0 -> x1, waiting for transfers between devices: none -> 67.7 us  [on_device(): every_stat = lax.psum(placed, 'grp')]
    all_to_all x3 -> x1, waiting for transfers between devices: 39.6 us -> 0.01 us  [on_device(): received = lax.all_to_all(blocks, 'grp', 0, 0, tiled=True)]
    all_to_all x1 -> x2, blocking collectives: 28.7 us -> 54.8 us  [reduce_blocks(): swapped = lax.all_to_all(blocks, axis, 0, 0, tiled=True)]
    all_to_all x3 -> x1, starting transfers between devices: 18.4 us -> 6.46 us  [on_device(): received = lax.all_to_all(blocks, 'grp', 0, 0, tiled=True)]
    reduce_sum x2 -> x3, other arithmetic: 1.2 us -> 5.6 us  [the longest x1 4.55 us: on_device(): row_total = jnp.sum(raised, axis=(1, 2))]
    unnamed x26 -> x22, local copies, waits for them, and re-layouts: 4.73 us -> 1.69 us
  transfers between devices with their start and end apart: 11 -> 10, of which waited for: 7 -> 5; matrix products, arithmetic and copies ran while one was open for 5% -> 7% of each run, Pallas kernels for 0% -> 0%
where the time goes in v6:
time: 275 us; the launch traced here: 274 us
  waiting for transfers between devices  129 us (47%)
  blocking collectives  54.8 us (20%)
  starting transfers between devices  36 us (13%)
  between operations  15.1 us (5%)
  other arithmetic  14.7 us (5%)
  matrix products  12.2 us (4%)
  local copies, waits for them, and re-layouts  12.1 us (4%)
    psum x1, waiting for transfers between devices, on_device(): every_stat = lax.psum(placed, 'grp')  67.7 us
    all_to_all x2, blocking collectives, reduce_blocks(): swapped = lax.all_to_all(blocks, axis, 0, 0, tiled=True)  54.8 us
    all_gather x1, waiting for transfers between devices, on_device(): every_block = lax.all_gather(captions, 'dp', axis=0, tiled=False)  50 us
    ppermute x7, starting transfers between devices, gather_ring(): received.append(lax.ppermute(part, axis, pairs))  29.2 us
    ppermute x7, waiting for transfers between devices, gather_ring(): received.append(lax.ppermute(part, axis, pairs))  10.6 us
    all_to_all x1, starting transfers between devices, on_device(): received = lax.all_to_all(blocks, 'grp', 0, 0, tiled=True)  6.46 us
  transfers between devices with their start and end apart: 10, of which 5 were waited for; matrix products, arithmetic and copies ran while one was open for 7% of the time, Pallas kernels for 0%

profile of v6, /device:TPU:1, one launch (start us, length us, event | category | flops | bytes accessed | tf_op | source)
XLA Modules:
  0.0 273.9 jit_solution(4231261601271892644)
XLA Ops:
  7.2 0.0 copy-start
  7.2 0.0 all-gather.3.cloned.1.call-start
  7.2 0.7 all-gather.3.cloned.1.call-update
  7.9 0.5 copy-done
  8.4 3.1 %multiply_multiply_fusion.2 = (f32[512,512]{1,0:T(8,128)S(1)}, f32[512,512]{1,0:T(8,128)}) fusion(bf16[512,1024]{1,0:T(8,128)(2,1)S(1)} %copy-done, bf16[1024,512]{1,0:T(8,128)(2,1)} %param.7), kind=kOutput, calls=%fused_computation.27 | convolution fusion | flops 538968064 | bytes 4194304 | tf_op jit(solution)/shard_map/dot_general | solution.py:39
  11.5 0.3 reshape.324
  11.8 0.6 reduce_sum.74
  12.4 0.1 multiply_reduce_fusion.1
  12.5 0.1 multiply_convert_fusion.1
  12.6 4.0 %collective-permute-start = (bf16[128,512]{1,0:T(8,128)(2,1)S(1)}, bf16[128,512]{1,0:T(8,128)(2,1)S(1)}, u32[]{:S(2)}, u32[]{:S(2)}) collective-permute-start(bf16[128,512]{1,0:T(8,128)(2,1)S(1)} %multiply_convert_fusion.1), channel_id=1, source_target_pairs={{0,1},{1,2},{2,3},{3,4},{4,5},{5,6},{6,7},{7,0},{8,9},{9,10},{10,1... | collective-permute-start | bytes 393224 | tf_op jit(solution)/shard_map/ppermute | solution.py:17
  16.7 4.2 %collective-permute-start.1 = (bf16[128,512]{1,0:T(8,128)(2,1)S(1)}, bf16[128,512]{1,0:T(8,128)(2,1)S(1)}, u32[]{:S(2)}, u32[]{:S(2)}) collective-permute-start(bf16[128,512]{1,0:T(8,128)(2,1)S(1)} %multiply_convert_fusion.1), channel_id=1, source_target_pairs={{0,2},{1,3},{2,4},{3,5},{4,6},{5,7},{6,0},{7,1},{8,10},{9,11},{10,... | collective-permute-start | bytes 393224 | tf_op jit(solution)/shard_map/ppermute | solution.py:17
  20.9 4.6 %collective-permute-start.2 = (bf16[128,512]{1,0:T(8,128)(2,1)S(1)}, bf16[128,512]{1,0:T(8,128)(2,1)S(1)}, u32[]{:S(2)}, u32[]{:S(2)}) collective-permute-start(bf16[128,512]{1,0:T(8,128)(2,1)S(1)} %multiply_convert_fusion.1), channel_id=1, source_target_pairs={{0,3},{1,4},{2,5},{3,6},{4,7},{5,0},{6,1},{7,2},{8,11},{9,12},{10,... | collective-permute-start | bytes 393224 | tf_op jit(solution)/shard_map/ppermute | solution.py:17
  25.6 3.5 %collective-permute-start.3 = (bf16[128,512]{1,0:T(8,128)(2,1)S(1)}, bf16[128,512]{1,0:T(8,128)(2,1)S(1)}, u32[]{:S(2)}, u32[]{:S(2)}) collective-permute-start(bf16[128,512]{1,0:T(8,128)(2,1)S(1)} %multiply_convert_fusion.1), channel_id=1, source_target_pairs={{0,4},{1,5},{2,6},{3,7},{4,0},{5,1},{6,2},{7,3},{8,12},{9,13},{10,... | collective-permute-start | bytes 393224 | tf_op jit(solution)/shard_map/ppermute | solution.py:17
  29.1 4.9 %collective-permute-start.4 = (bf16[128,512]{1,0:T(8,128)(2,1)S(1)}, bf16[128,512]{1,0:T(8,128)(2,1)S(1)}, u32[]{:S(2)}, u32[]{:S(2)}) collective-permute-start(bf16[128,512]{1,0:T(8,128)(2,1)S(1)} %multiply_convert_fusion.1), channel_id=1, source_target_pairs={{0,5},{1,6},{2,7},{3,0},{4,1},{5,2},{6,3},{7,4},{8,13},{9,14},{10,... | collective-permute-start | bytes 393224 | tf_op jit(solution)/shard_map/ppermute | solution.py:17
  34.0 0.6 dynamic_slice.21
  34.6 0.2 fusion.28
  34.8 0.7 gather_fusion.1
  36.2 0.1 compare_and_fusion
  36.3 0.1 broadcast_bitcast_fusion
  36.4 0.1 fusion.26
  36.4 0.1 fusion.38
  36.5 0.0 collective-permute-done
  36.5 5.0 %collective-permute-start.5 = (bf16[128,512]{1,0:T(8,128)(2,1)S(1)}, bf16[128,512]{1,0:T(8,128)(2,1)S(1)}, u32[]{:S(2)}, u32[]{:S(2)}) collective-permute-start(bf16[128,512]{1,0:T(8,128)(2,1)S(1)} %multiply_convert_fusion.1), channel_id=1, source_target_pairs={{0,6},{1,7},{2,0},{3,1},{4,2},{5,3},{6,4},{7,5},{8,14},{9,15},{10,... | collective-permute-start | bytes 393224 | tf_op jit(solution)/shard_map/ppermute | solution.py:17
  41.5 3.0 %collective-permute-start.6 = (bf16[128,512]{1,0:T(8,128)(2,1)S(1)}, bf16[128,512]{1,0:T(8,128)(2,1)S(1)}, u32[]{:S(2)}, u32[]{:S(2)}) collective-permute-start(bf16[128,512]{1,0:T(8,128)(2,1)S(1)} %multiply_convert_fusion.1), channel_id=1, source_target_pairs={{0,7},{1,0},{2,1},{3,2},{4,3},{5,4},{6,5},{7,6},{8,15},{9,8},{10,9... | collective-permute-start | bytes 393224 | tf_op jit(solution)/shard_map/ppermute | solution.py:17
  44.6 0.4 collective-permute-done.4
  45.0 6.8 %collective-permute-done.5 = bf16[128,512]{1,0:T(8,128)(2,1)S(1)} collective-permute-done((bf16[128,512]{1,0:T(8,128)(2,1)S(1)}, bf16[128,512]{1,0:T(8,128)(2,1)S(1)}, u32[]{:S(2)}, u32[]{:S(2)}) %collective-permute-start.5) | collective-permute-done | bytes 131104 | tf_op jit(solution)/shard_map/ppermute | solution.py:17
  51.9 3.3 %collective-permute-done.6 = bf16[128,512]{1,0:T(8,128)(2,1)S(1)} collective-permute-done((bf16[128,512]{1,0:T(8,128)(2,1)S(1)}, bf16[128,512]{1,0:T(8,128)(2,1)S(1)}, u32[]{:S(2)}, u32[]{:S(2)}) %collective-permute-start.6) | collective-permute-done | bytes 131104 | tf_op jit(solution)/shard_map/ppermute | solution.py:17
  55.2 0.6 gather_fusion
  55.8 1.3 bitcast_select_fusion
  57.1 50.0 %all-gather.3.cloned.1.call-done = bf16[8192,512]{1,0:T(8,128)(2,1)} async-done(((bf16[128,512]{1,0:T(8,128)(2,1)}), bf16[8192,512]{1,0:T(8,128)(2,1)}) %all-gather.3.cloned.1.call-update) | async-done | bytes 8388624 | tf_op jit(solution)/shard_map/all_gather | solution.py:38
  107.1 4.1 %gather_fusion.2 = bf16[16,128,512]{2,1,0:T(8,128)(2,1)S(1)} fusion(bf16[64,128,512]{2,1,0:T(8,128)(2,1)} %bitcast.83, s32[1024]{0:T(1024)S(1)} %pad_clamp_fusion), kind=kCustom, calls=%fused_computation.2 | custom fusion | bytes 4194368 | tf_op jit(solution)/shard_map/jit(_take)/gather | solution.py:50
  111.2 0.3 broadcast_select_fusion
  111.5 0.9 copy-done.4
  112.4 2.5 fusion.46
  114.9 4.2 %fusion.47 = (bf16[1024,512]{1,0:T(8,128)(2,1)}, f32[1024,512]{1,0:T(8,128)}) fusion(bf16[16,128,512]{2,1,0:T(8,128)(2,1)S(1)} %broadcast_select_fusion, f32[1024,16,128]{0,2,1:T(8,128)S(1)} %get-tuple-element.12, f32[1024]{0:T(1024)S(1)} %get-tuple-element.11), kind=kOutput, calls=%fused_computation.105 | convolution fusion | flops 2152202240 | bytes 13635584 | tf_op jit(solution)/shard_map/rsc,sce->re/dot_general | solution.py:59
  119.1 6.5 %all-to-all-start = ((bf16[8,128,512]{2,1,0:T(8,128)(2,1)}), bf16[8,128,512]{2,1,0:T(8,128)(2,1)S(1)}, u32[]{:S(2)}, u32[]{:S(2)}) async-start(bf16[8,128,512]{2,1,0:T(8,128)(2,1)} %bitcast.28), calls=%async_computation | async-start | bytes 2097152 | tf_op jit(solution)/shard_map/all_to_all | solution.py:66
  125.6 0.2 all-reduce.2.cloned.1.call-start
  125.8 1.1 slice.24
  126.9 4.6 %fusion.1 = f32[1024]{0:T(1024)S(1)} fusion(f32[1024,16,128]{0,2,1:T(8,128)} %copy-done.2, f32[1024]{0:T(1024)S(1)} %get-tuple-element.11), kind=kLoop, calls=%fused_computation.7 | loop fusion | flops 4193280 | bytes 8396800 | tf_op jit(solution)/shard_map/reduce_sum | solution.py:58
  131.5 0.7 broadcast_select_fusion.1
  132.2 0.0 all-reduce.2.cloned.1.call-update
  132.2 1.3 gather_fusion.3
  133.5 67.7 %all-reduce.2.cloned.1.call-done = f32[8,2,1024]{2,0,1:T(8,128)} async-done(((f32[8,2,1024]{2,0,1:T(8,128)}), f32[8,2,1024]{2,0,1:T(8,128)}) %all-reduce.2.cloned.1.call-update) | async-done | bytes 65552 | tf_op jit(solution)/shard_map/psum | solution.py:64
  201.2 0.7 dynamic-slice_reduce_fusion
  201.9 0.7 fusion.30
  202.6 0.5 fusion.45
  203.1 0.7 fusion.32
  203.8 1.1 fusion.27
  204.9 0.3 select_reduce_fusion
  205.3 0.2 multiply_reduce_fusion
  205.5 0.8 broadcast_multiply_fusion
  206.3 0.2 broadcast_in_dim.110
  206.5 0.4 reshape.326
  206.9 2.5 fusion.8
  209.3 0.5 copy.15
  209.9 44.2 %all_to_all.15 = bf16[64,16,512]{2,1,0:T(8,128)(2,1)S(1)} all-to-all(bf16[64,16,512]{2,1,0:T(8,128)(2,1)S(1)} %bitcast.82), channel_id=1, replica_groups=mesh['dp'=64,'grp'=8] {'dp'}, dimensions={0} | all-to-all | bytes 2097152 | tf_op jit(solution)/shard_map/all_to_all | solution.py:24
  254.1 0.2 convert_reduce_fusion
  254.3 0.1 reshape.328
  254.4 0.1 reshape.364
  254.5 10.6 %all_to_all.16 = f32[8,1,1024]{2,1,0:T(1,128)S(1)} all-to-all(f32[8,1,1024]{2,1,0:T(1,128)S(1)} %reshape.364), channel_id=1, replica_groups=mesh['dp'=64,'grp'=8] {'grp'}, dimensions={0} | all-to-all | bytes 65536 | tf_op jit(solution)/shard_map/all_to_all | solution.py:24
  265.1 0.5 broadcast.324
  265.6 0.7 reduce.3
  266.3 0.1 reshape.365
  266.4 0.6 reduce_sum.82
  (37 shorter events, 0.3 us)
Async XLA Ops:
  7.2 1.2 copy-start
  7.2 99.9 %all-gather.3.cloned.1.call-start = ((), (), s32[]{:S(2)}) async-start(), calls=%async_computation.4 | async-start | bytes 8519680 | tf_op jit(solution)/shard_map/all_gather | solution.py:38
  11.5 22.5 %copy-start.6 = (s32[64]{0:T(128)S(1)}, s32[64]{0:T(128)}, u32[]{:S(2)}) copy-start(s32[64]{0:T(128)} %param.11) | copy-start | bytes 772
  11.5 23.1 %copy-start.5 = (s32[64,14]{0,1:T(8,128)S(1)}, s32[64,14]{0,1:T(8,128)}, u32[]{:S(2)}) copy-start(s32[64,14]{0,1:T(8,128)} %param.10) | copy-start | bytes 10756
  11.5 23.3 %copy-start.1 = (s32[64]{0:T(128)S(1)}, s32[64]{0:T(128)}, u32[]{:S(2)}) copy-start(s32[64]{0:T(128)} %param.9) | copy-start | bytes 772
  12.6 23.9 %collective-permute-start = (bf16[128,512]{1,0:T(8,128)(2,1)S(1)}, bf16[128,512]{1,0:T(8,128)(2,1)S(1)}, u32[]{:S(2)}, u32[]{:S(2)}) collective-permute-start(bf16[128,512]{1,0:T(8,128)(2,1)S(1)} %multiply_convert_fusion.1), channel_id=1, source_target_pairs={{0,1},{1,2},{2,3},{3,4},{4,5},{5,6},{6,7},{7,0},{8,9},{9,10},{10,1... | collective-permute-start | bytes 393224 | tf_op jit(solution)/shard_map/ppermute | solution.py:17
  16.7 24.8 %collective-permute-start.1 = (bf16[128,512]{1,0:T(8,128)(2,1)S(1)}, bf16[128,512]{1,0:T(8,128)(2,1)S(1)}, u32[]{:S(2)}, u32[]{:S(2)}) collective-permute-start(bf16[128,512]{1,0:T(8,128)(2,1)S(1)} %multiply_convert_fusion.1), channel_id=1, source_target_pairs={{0,2},{1,3},{2,4},{3,5},{4,6},{5,7},{6,0},{7,1},{8,10},{9,11},{10,... | collective-permute-start | bytes 393224 | tf_op jit(solution)/shard_map/ppermute | solution.py:17
  20.9 23.6 %collective-permute-start.2 = (bf16[128,512]{1,0:T(8,128)(2,1)S(1)}, bf16[128,512]{1,0:T(8,128)(2,1)S(1)}, u32[]{:S(2)}, u32[]{:S(2)}) collective-permute-start(bf16[128,512]{1,0:T(8,128)(2,1)S(1)} %multiply_convert_fusion.1), channel_id=1, source_target_pairs={{0,3},{1,4},{2,5},{3,6},{4,7},{5,0},{6,1},{7,2},{8,11},{9,12},{10,... | collective-permute-start | bytes 393224 | tf_op jit(solution)/shard_map/ppermute | solution.py:17
  25.6 19.0 %collective-permute-start.3 = (bf16[128,512]{1,0:T(8,128)(2,1)S(1)}, bf16[128,512]{1,0:T(8,128)(2,1)S(1)}, u32[]{:S(2)}, u32[]{:S(2)}) collective-permute-start(bf16[128,512]{1,0:T(8,128)(2,1)S(1)} %multiply_convert_fusion.1), channel_id=1, source_target_pairs={{0,4},{1,5},{2,6},{3,7},{4,0},{5,1},{6,2},{7,3},{8,12},{9,13},{10,... | collective-permute-start | bytes 393224 | tf_op jit(solution)/shard_map/ppermute | solution.py:17
  29.1 15.9 %collective-permute-start.4 = (bf16[128,512]{1,0:T(8,128)(2,1)S(1)}, bf16[128,512]{1,0:T(8,128)(2,1)S(1)}, u32[]{:S(2)}, u32[]{:S(2)}) collective-permute-start(bf16[128,512]{1,0:T(8,128)(2,1)S(1)} %multiply_convert_fusion.1), channel_id=1, source_target_pairs={{0,5},{1,6},{2,7},{3,0},{4,1},{5,2},{6,3},{7,4},{8,13},{9,14},{10,... | collective-permute-start | bytes 393224 | tf_op jit(solution)/shard_map/ppermute | solution.py:17
  36.5 15.3 %collective-permute-start.5 = (bf16[128,512]{1,0:T(8,128)(2,1)S(1)}, bf16[128,512]{1,0:T(8,128)(2,1)S(1)}, u32[]{:S(2)}, u32[]{:S(2)}) collective-permute-start(bf16[128,512]{1,0:T(8,128)(2,1)S(1)} %multiply_convert_fusion.1), channel_id=1, source_target_pairs={{0,6},{1,7},{2,0},{3,1},{4,2},{5,3},{6,4},{7,5},{8,14},{9,15},{10,... | collective-permute-start | bytes 393224 | tf_op jit(solution)/shard_map/ppermute | solution.py:17
  41.5 13.7 %collective-permute-start.6 = (bf16[128,512]{1,0:T(8,128)(2,1)S(1)}, bf16[128,512]{1,0:T(8,128)(2,1)S(1)}, u32[]{:S(2)}, u32[]{:S(2)}) collective-permute-start(bf16[128,512]{1,0:T(8,128)(2,1)S(1)} %multiply_convert_fusion.1), channel_id=1, source_target_pairs={{0,7},{1,0},{2,1},{3,2},{4,3},{5,4},{6,5},{7,6},{8,15},{9,8},{10,9... | collective-permute-start | bytes 393224 | tf_op jit(solution)/shard_map/ppermute | solution.py:17
  111.2 1.2 copy-start.4
  112.4 2.5 copy-start.3
  114.9 4.2 %copy-start.2 = (f32[1024,16,128]{0,2,1:T(8,128)}, f32[1024,16,128]{0,2,1:T(8,128)S(1)}, u32[]{:S(2)}) copy-start(f32[1024,16,128]{0,2,1:T(8,128)S(1)} %get-tuple-element.12) | copy-start | bytes 25165828
  119.1 85.8 %all-to-all-start = ((bf16[8,128,512]{2,1,0:T(8,128)(2,1)}), bf16[8,128,512]{2,1,0:T(8,128)(2,1)S(1)}, u32[]{:S(2)}, u32[]{:S(2)}) async-start(bf16[8,128,512]{2,1,0:T(8,128)(2,1)} %bitcast.28), calls=%async_computation | async-start | bytes 2097152 | tf_op jit(solution)/shard_map/all_to_all | solution.py:66
  125.6 75.6 %all-reduce.2.cloned.1.call-start = ((), (), s32[]{:S(2)}) async-start(), calls=%async_computation.3 | async-start | bytes 131072 | tf_op jit(solution)/shard_map/psum | solution.py:64
Sparse Core Ops, SparseCore 0:
  11.4 95.6 all-gather.2
  132.3 68.8 all-reduce.1
